TPU v7x, 256 devices: a whole 4x4x8 slice. The times are simulated.
256 devices in a mesh: dp: 8 (over z), expert: 32 (over y, x, core).
Axes of the slice: x: 4, y: 4, z: 8, core: 2. Of those that a mesh axis runs over, the one named last changes fastest.
Arguments:
- hidden_in: bfloat16 [16384, 2560], P(('dp', 'expert')), may hold values from -420 to 420
- norm_gain: float32 [2560], replicated, may hold values from 0.25 to 1.75
- expert_ids: int32 [16384, 6], P(('dp', 'expert')), may hold values from 0 to 63, all different within a row; in each aligned block of 64 rows (0 to 63, 64 to 127, ...) at most 7 rows name the same one
- gate_weights: bfloat16 [16384, 6], P(('dp', 'expert')), may hold values from 0.049804688 to 0.5
- expert_slot: int32 [64], replicated, may hold values from 0 to 63, each once
- w_in: bfloat16 [64, 2560, 3072], P('expert', None, 'dp'), may hold values from -0.125 to 0.125
- w_down: bfloat16 [64, 1536, 2560], P('expert', 'dp'), may hold values from -0.15625 to 0.15625
- shared_in: bfloat16 [2560, 6144], P(None, 'dp'), may hold values from -0.125 to 0.125
- shared_down: bfloat16 [3072, 2560], P('dp'), may hold values from -0.109375 to 0.109375
Outputs:
- mixed: bfloat16 [16384, 2560], P(('dp', 'expert'))
Inputs may be any that keep to these rules, and one draw needn't show every extreme that they name: `expert_ids`: each token names 6 different experts; among the tokens of one device no expert is named by more than 7. `expert_slot`: each slot holds exactly one expert.
All inputs are finite; a program needn't handle non-finite values.
Results may differ from a plain program's by a relative error of at most 0.0085.
Values may be sent and summed in bfloat16 or wider, within the bound.
No kernel may reach another device: no remote copies, remote signals or barrier semaphores. Data moves between devices by JAX's collectives and lax.ppermute only.
A program may use at most 192 MiB of HBM per device.

v0:
```python
import jax
import jax.numpy as jnp
from jax import lax
from jax.sharding import PartitionSpec as P

epsilon = 1e-06


def normalize(hidden, gain):
    widened = hidden.astype(jnp.float32)
    mean_square = jnp.mean(widened * widened, axis=-1, keepdims=True)
    return (widened * lax.rsqrt(mean_square + epsilon) * gain).astype(jnp.bfloat16)


def on_device(
    hidden_in,
    norm_gain,
    expert_ids,
    gate_weights,
    expert_slot,
    w_in,
    w_down,
    shared_in,
    shared_down,
):
    groups = lax.axis_size("dp")
    columns = lax.axis_size("expert")
    local_experts = w_in.shape[0]
    experts = local_experts * columns
    token_count = hidden_in.shape[0]
    top_count = expert_ids.shape[1]
    model_width = hidden_in.shape[1]
    capacity = max(2, token_count * top_count * 7 // (6 * experts))
    row_total = groups * token_count
    normed = normalize(hidden_in, norm_gain)
    gathered, all_routes, all_gates = (
        lax.all_gather(normed, "dp", axis=0, tiled=True),
        lax.all_gather(expert_ids, "dp", axis=0, tiled=True),
        lax.all_gather(gate_weights, "dp", axis=0, tiled=True),
    )
    shared_width = shared_down.shape[0]
    shared_both = jnp.dot(gathered, shared_in, preferred_element_type=jnp.float32)
    shared_act = (
        jax.nn.silu(shared_both[:, :shared_width]) * shared_both[:, shared_width:]
    ).astype(jnp.bfloat16)
    shared_part = jnp.dot(shared_act, shared_down, preferred_element_type=jnp.float32).astype(
        jnp.bfloat16
    )
    block_routes = all_routes.reshape(groups, token_count * top_count)
    onehot = block_routes[:, :, None] == jnp.arange(experts, dtype=jnp.int32)[None, None, :]
    onehot_int = onehot.astype(jnp.int32)
    slot_rank = jnp.sum(jnp.cumsum(onehot_int, axis=1) * onehot_int, axis=2) - 1
    slot_of = jnp.sum(jnp.where(onehot, expert_slot[None, None, :], 0), axis=2)
    own_slots = slot_of * capacity + slot_rank
    flat_index = jnp.arange(groups, dtype=jnp.int32)[:, None] * (experts * capacity) + own_slots
    source_row = jnp.repeat(jnp.arange(row_total, dtype=jnp.int32), top_count)
    row_table = (
        jnp.full((groups * experts * capacity,), row_total, jnp.int32)
        .at[flat_index.reshape(-1)]
        .set(source_row)
    )
    padded = jnp.concatenate([gathered, jnp.zeros((1, model_width), jnp.bfloat16)], axis=0)
    outgoing = padded[row_table].reshape(groups, columns, local_experts, capacity, model_width)
    received = lax.all_to_all(outgoing, "expert", split_axis=1, concat_axis=1, tiled=True)
    slice_width = w_down.shape[1]
    gate_up = jnp.einsum("bslcd,ldf->bslcf", received, w_in, preferred_element_type=jnp.float32)
    activated = (jax.nn.silu(gate_up[..., :slice_width]) * gate_up[..., slice_width:]).astype(
        jnp.bfloat16
    )
    partial_value = jnp.einsum(
        "bslcf,lfd->bslcd", activated, w_down, preferred_element_type=jnp.float32
    ).astype(jnp.bfloat16)
    returned = lax.all_to_all(partial_value, "expert", split_axis=1, concat_axis=1, tiled=True)
    picked = returned.reshape(-1, model_width)[flat_index.reshape(-1)].reshape(
        row_total, top_count, model_width
    )
    routed = jnp.sum(all_gates.astype(jnp.float32)[:, :, None] * picked.astype(jnp.float32), axis=1)
    term_sum = routed + shared_part.astype(jnp.float32)
    mixed = lax.psum_scatter(term_sum, "dp", scatter_dimension=0, tiled=True)
    return mixed.astype(jnp.bfloat16)


def solution(mesh):
    return jax.shard_map(
        on_device,
        mesh=mesh,
        in_specs=(
            P(("dp", "expert"), None),
            P(),
            P(("dp", "expert"), None),
            P(("dp", "expert"), None),
            P(),
            P("expert", None, "dp"),
            P("expert", "dp", None),
            P(None, "dp"),
            P("dp", None),
        ),
        out_specs=P(("dp", "expert"), None),
        check_vma=False,
    )
```

profile of v0, /device:TPU:1, one launch (start us, length us, event | category | flops | bytes accessed | tf_op | source)
XLA Modules:
  0.0 877.1 jit_solution(11710927405017402053)
XLA Ops:
  6.5 1.3 fusion.15
  7.8 1.9 fusion.17
  9.7 23.3 %all-gather.1 = s32[8,64,6]{1,2,0:T(8,128)S(1)} all-gather(s32[1,64,6]{1,2,0:T(8,128)} %bitcast.51), channel_id=1, replica_groups=mesh['dp'=8,'expert'=32] {'dp'}, dimensions={0}, use_global_device_ids=true | all-gather | bytes 13824 | tf_op jit(solution)/shard_map/all_gather | solution.py:38
  33.4 0.2 eq.29
  33.6 0.8 reshape.118
  34.4 7.2 reduce-window.6
  41.6 0.3 slice.28
  41.9 0.9 copy.45
  42.8 0.7 fusion.20
  43.5 0.4 select_reduce_fusion
  44.0 12.0 %scatter_custom_fusion = s32[3584]{0:T(1024)S(1)} fusion(s32[3072]{0:T(1024)S(1)} %bitcast.48, s32[3072]{0:T(1024)} %reshape.118, s32[]{:T(128)} %constant.8.clone.1), kind=kCustom, calls=%fused_computation.38 | custom fusion | bytes 14848 | tf_op jit(solution)/shard_map/scatter | solution.py:60
  56.0 3.4 concatenate.3
  59.5 35.2 %gather_fusion = bf16[3584,2560]{1,0:T(8,128)(2,1)} fusion(bf16[513,2560]{1,0:T(8,128)(2,1)} %concatenate.3, s32[4096]{0:T(1024)S(1)} %pad_clamp_fusion), kind=kCustom, calls=%fused_computation | custom fusion | bytes 36714496 | tf_op jit(solution)/shard_map/gather | solution.py:63
  94.7 25.8 %reshape.95 = bf16[8,32,2,7,2560]{4,3,2,1,0:T(8,128)(2,1)} reshape(bf16[3584,2560]{1,0:T(8,128)(2,1)} %gather_fusion) | data formatting | bytes 36700160 | tf_op jit(solution)/shard_map/reshape | solution.py:63
  120.5 18.6 %copy.48 = bf16[8,32,2,7,2560]{4,0,3,2,1:T(8,128)(2,1)S(1)} copy(bf16[8,32,2,7,2560]{4,3,2,1,0:T(8,128)(2,1)} %reshape.95) | data formatting | bytes 36700160 | tf_op jit(solution)/shard_map/reshape | solution.py:63
  139.1 216.2 %all_to_all.10 = bf16[8,32,2,7,2560]{4,0,3,2,1:T(8,128)(2,1)} all-to-all(bf16[8,32,2,7,2560]{4,0,3,2,1:T(8,128)(2,1)S(1)} %copy.48), channel_id=1, replica_groups=mesh['dp'=8,'expert'=32] {'expert'}, dimensions={1} | all-to-all | bytes 36700160 | tf_op jit(solution)/shard_map/all_to_all | solution.py:64
  355.3 14.3 %fusion.4 = f32[8,32,2,7,384]{4,0,3,1,2:T(8,128)S(1)} fusion(bf16[2,2560,384]{2,1,0:T(8,128)(2,1)} %param.14, bf16[8,32,2,7,2560]{4,0,3,2,1:T(8,128)(2,1)} %all_to_all.10), kind=kOutput, calls=%fused_computation.12 | convolution fusion | flops 7046430720 | bytes 27787264 | tf_op jit(solution)/shard_map/bslcd,ldf->bslcf/dot_general | solution.py:66
  369.6 1.1 fusion.3
  370.7 8.8 %convert_bitcast_fusion = bf16[8,32,2,7,2560]{4,1,3,0,2:T(8,128)(2,1)} fusion(bf16[2,192,2560]{2,1,0:T(8,128)(2,1)S(1)} %copy-done, bf16[8,32,2,7,192]{4,0,3,1,2:T(8,128)(2,1)S(1)} %fusion.3), kind=kOutput, calls=%fused_computation.6 | convolution fusion | flops 3532390400 | bytes 21692416 | tf_op jit(solution)/shard_map/bslcf,lfd->bslcd/dot_general | solution.py:70
  379.5 20.6 %copy.51 = bf16[8,32,2,7,2560]{4,0,3,2,1:T(8,128)(2,1)} copy(bf16[8,32,2,7,2560]{4,1,3,0,2:T(8,128)(2,1)} %convert_bitcast_fusion) | data formatting | bytes 36700160 | tf_op jit(solution)/shard_map/convert_element_type | solution.py:72
  400.1 5.3 all-to-all-start.1
  405.5 18.7 %all-gather = bf16[8,64,6]{1,2,0:T(8,128)(2,1)S(1)} all-gather(bf16[1,64,6]{1,2,0:T(8,128)(2,1)S(1)} %bitcast.52), channel_id=1, replica_groups=mesh['dp'=8,'expert'=32] {'dp'}, dimensions={0}, use_global_device_ids=true | all-gather | bytes 6912 | tf_op jit(solution)/shard_map/all_gather | solution.py:39
  424.4 6.3 fusion.25
  430.7 195.8 %all-to-all-done.1 = bf16[8,32,2,7,2560]{4,0,3,2,1:T(8,128)(2,1)} async-done(((bf16[8,32,2,7,2560]{4,0,3,2,1:T(8,128)(2,1)}), bf16[8,32,2,7,2560]{4,0,3,2,1:T(8,128)(2,1)}, u32[]{:S(2)}, u32[]{:S(2)}) %all-to-all-start.1) | async-done | bytes 18350112 | tf_op jit(solution)/shard_map/all_to_all | solution.py:73
  626.5 19.6 %copy.52 = bf16[8,32,2,7,2560]{4,3,2,1,0:T(8,128)(2,1)} copy(bf16[8,32,2,7,2560]{4,0,3,2,1:T(8,128)(2,1)} %all-to-all-done.1) | data formatting | bytes 36700160 | tf_op jit(solution)/shard_map/all_to_all | solution.py:73
  646.2 26.1 %reshape.96 = bf16[3584,2560]{1,0:T(8,128)(2,1)} reshape(bf16[8,32,2,7,2560]{4,3,2,1,0:T(8,128)(2,1)} %copy.52) | data formatting | bytes 36700160 | tf_op jit(solution)/shard_map/reshape | solution.py:74
  672.2 37.2 %gather_fusion.1 = bf16[3072,2560]{1,0:T(8,128)(2,1)} fusion(bf16[3584,2560]{1,0:T(8,128)(2,1)} %reshape.96, s32[3072]{0:T(1024)S(1)} %broadcast_clamp_fusion), kind=kCustom, calls=%fused_computation.1 | custom fusion | bytes 31469568 | tf_op jit(solution)/shard_map/gather | solution.py:74
  709.4 27.2 %reshape.97 = f32[512,6,2560]{2,1,0:T(8,128)} reshape(bf16[3072,2560]{1,0:T(8,128)(2,1)} %gather_fusion.1) | data formatting | bytes 47185920 | tf_op jit(solution)/shard_map/convert_element_type | solution.py:77
  736.6 54.1 %multiply_reduce_fusion = f32[512,2560]{1,0:T(8,128)S(1)} fusion(f32[512,6,2560]{2,1,0:T(8,128)} %reshape.97, f32[512,6]{1,0:T(8,128)S(1)} %bitcast.47), kind=kLoop, calls=%fused_computation.3 | loop fusion | flops 14417920 | bytes 36712448 | tf_op jit(solution)/shard_map/reduce_sum | solution.py:77
  790.8 5.4 convert_add_fusion
  796.2 72.3 %reduce-scatter.2.cloned.1.call-done = f32[64,2560]{1,0:T(8,128)} async-done(((f32[512,2560]{1,0:T(8,128)}), f32[64,2560]{1,0:T(8,128)}) %reduce-scatter.2.cloned.1.call-update) | async-done | bytes 655376 | tf_op jit(solution)/shard_map/reduce_scatter | solution.py:79
  868.4 1.8 convert_element_type.53
  (31 shorter events, 0.8 us)
Async XLA Ops:
  6.5 364.1 %copy-start = (bf16[2,192,2560]{2,1,0:T(8,128)(2,1)S(1)}, bf16[2,192,2560]{2,1,0:T(8,128)(2,1)}, u32[]{:S(2)}) copy-start(bf16[2,192,2560]{2,1,0:T(8,128)(2,1)} %param.15) | copy-start | bytes 5898244
  6.5 37.0 %copy-start.4 = (s32[64]{0:T(128)S(1)}, s32[64]{0:T(128)}, u32[]{:S(2)}) copy-start(s32[64]{0:T(128)} %param.13) | copy-start | bytes 772
  6.5 49.5 %all-gather.4.cloned.1.call-start = ((), (), s32[]{:S(2)}) async-start(), calls=%async_computation.3 | async-start | bytes 2949120 | tf_op jit(solution)/shard_map/all_gather | solution.py:37
  400.1 5.4 copy-start.3
  400.1 226.4 %all-to-all-start.1 = ((bf16[8,32,2,7,2560]{4,0,3,2,1:T(8,128)(2,1)}), bf16[8,32,2,7,2560]{4,0,3,2,1:T(8,128)(2,1)}, u32[]{:S(2)}, u32[]{:S(2)}) async-start(bf16[8,32,2,7,2560]{4,0,3,2,1:T(8,128)(2,1)} %copy.51), calls=%async_computation.1 | async-start | bytes 36700160 | tf_op jit(solution)/shard_map/all_to_all | solution.py:73
  405.4 463.0 %reduce-scatter.2.cloned.1.call-start = ((), (), s32[]{:S(2)}) async-start(), calls=%async_computation.4 | async-start | bytes 5898240 | tf_op jit(solution)/shard_map/reduce_scatter | solution.py:79
  736.6 54.1 %copy-start.2 = (bf16[384,2560]{1,0:T(8,128)(2,1)S(1)}, bf16[384,2560]{1,0:T(8,128)(2,1)}, u32[]{:S(2)}) copy-start(bf16[384,2560]{1,0:T(8,128)(2,1)} %param.17) | copy-start | bytes 5898244
  790.7 79.5 %copy-start.1 = (bf16[2,192,2560]{2,1,0:T(8,128)(2,1)S(1)}, bf16[2,192,2560]{2,1,0:T(8,128)(2,1)}, u32[]{:S(2)}) copy-start(bf16[2,192,2560]{2,1,0:T(8,128)(2,1)} %param.15) | copy-start | bytes 5898244
Sparse Core Ops, SparseCore 0:
  9.8 43.0 all-gather.3
  796.3 72.0 reduce-scatter.1
where the time goes:
time: 880 us; the launch traced here: 877 us
  waiting for transfers between devices  268 us (30%)
  blocking collectives  258 us (29%)
  local copies, waits for them, and re-layouts  228 us (26%)
  other arithmetic  68.6 us (8%)
  matrix products  34.8 us (4%)
  between operations  13.6 us (2%)
    all_to_all x1, blocking collectives, on_device(): lax.all_to_all(outgoing, 'expert', split_axis=1, concat_axis=1, tiled=True)  216 us
    all_to_all x1, waiting for transfers between devices, on_device(): lax.all_to_all(partial_value, 'expert', split_axis=1, concat_axis=1, tile...  196 us
    reduce_scatter x1, waiting for transfers between devices, on_device(): mixed = lax.psum_scatter(term_sum, 'dp', scatter_dimension=0, tiled=True)  72.3 us
    reduce_sum x1, other arithmetic, on_device(): jnp.sum(all_gates.astype(jnp.float32)[:, :, None] * picked.astype(jnp.flo...  54.1 us
    reshape x2, local copies, waits for them, and re-layouts, on_device(): padded[row_table]  44.4 us
    gather x1, local copies, waits for them, and re-layouts, on_device(): returned.reshape(-1, model_width)[flat_index.reshape(-1)]  37.2 us
    gather x1, local copies, waits for them, and re-layouts, on_device(): padded[row_table]  35.2 us
    convert_element_type x1, local copies, waits for them, and re-layouts, on_device(): picked.astype(jnp.float32)  27.2 us
  transfers between devices with their start and end apart: 3, of which 2 were waited for; matrix products, arithmetic and copies ran while one was open for 3% of the time, Pallas kernels for 0%

commit v1 on v0

--- a/solution.py
+++ b/solution.py
@@ -29,7 +29,6 @@
     experts = local_experts * columns
     token_count = hidden_in.shape[0]
     top_count = expert_ids.shape[1]
-    model_width = hidden_in.shape[1]
     capacity = max(2, token_count * top_count * 7 // (6 * experts))
     row_total = groups * token_count
     normed = normalize(hidden_in, norm_gain)
@@ -51,32 +50,35 @@
     onehot_int = onehot.astype(jnp.int32)
     slot_rank = jnp.sum(jnp.cumsum(onehot_int, axis=1) * onehot_int, axis=2) - 1
     slot_of = jnp.sum(jnp.where(onehot, expert_slot[None, None, :], 0), axis=2)
-    own_slots = slot_of * capacity + slot_rank
-    flat_index = jnp.arange(groups, dtype=jnp.int32)[:, None] * (experts * capacity) + own_slots
-    source_row = jnp.repeat(jnp.arange(row_total, dtype=jnp.int32), top_count)
-    row_table = (
-        jnp.full((groups * experts * capacity,), row_total, jnp.int32)
-        .at[flat_index.reshape(-1)]
-        .set(source_row)
-    )
-    padded = jnp.concatenate([gathered, jnp.zeros((1, model_width), jnp.bfloat16)], axis=0)
-    outgoing = padded[row_table].reshape(groups, columns, local_experts, capacity, model_width)
-    received = lax.all_to_all(outgoing, "expert", split_axis=1, concat_axis=1, tiled=True)
+    dest_col = slot_of // local_experts
+    local_of = slot_of % local_experts
+    group_of = jnp.arange(groups, dtype=jnp.int32)[:, None]
+    position = ((dest_col * groups + group_of) * capacity + slot_rank).reshape(row_total, top_count)
+    local_of = local_of.reshape(row_total, top_count)
+    buffer_rows = columns * groups * capacity
+    row_iota = jnp.arange(buffer_rows, dtype=jnp.int32)[None, None, :]
     slice_width = w_down.shape[1]
-    gate_up = jnp.einsum("bslcd,ldf->bslcf", received, w_in, preferred_element_type=jnp.float32)
-    activated = (jax.nn.silu(gate_up[..., :slice_width]) * gate_up[..., slice_width:]).astype(
-        jnp.bfloat16
-    )
-    partial_value = jnp.einsum(
-        "bslcf,lfd->bslcd", activated, w_down, preferred_element_type=jnp.float32
-    ).astype(jnp.bfloat16)
-    returned = lax.all_to_all(partial_value, "expert", split_axis=1, concat_axis=1, tiled=True)
-    picked = returned.reshape(-1, model_width)[flat_index.reshape(-1)].reshape(
-        row_total, top_count, model_width
-    )
-    routed = jnp.sum(all_gates.astype(jnp.float32)[:, :, None] * picked.astype(jnp.float32), axis=1)
-    term_sum = routed + shared_part.astype(jnp.float32)
-    mixed = lax.psum_scatter(term_sum, "dp", scatter_dimension=0, tiled=True)
+    routed = shared_part.astype(jnp.float32)
+    for local in range(local_experts):
+        hit = (position[:, :, None] == row_iota) & (local_of[:, :, None] == local)
+        dispatch = jnp.any(hit, axis=1).astype(jnp.bfloat16)
+        combine = jnp.sum(
+            jnp.where(hit, all_gates[:, :, None], jnp.zeros((), jnp.bfloat16)), axis=1
+        ).astype(jnp.bfloat16)
+        outgoing = lax.dot_general(
+            dispatch, gathered, (((0,), (0,)), ((), ())), preferred_element_type=jnp.float32
+        ).astype(jnp.bfloat16)
+        received = lax.all_to_all(outgoing, "expert", 0, 0, tiled=True)
+        gate_up = jnp.dot(received, w_in[local], preferred_element_type=jnp.float32)
+        activated = (
+            jax.nn.silu(gate_up[:, :slice_width]) * gate_up[:, slice_width:]
+        ).astype(jnp.bfloat16)
+        partial_value = jnp.dot(activated, w_down[local], preferred_element_type=jnp.float32).astype(
+            jnp.bfloat16
+        )
+        returned = lax.all_to_all(partial_value, "expert", 0, 0, tiled=True)
+        routed = routed + jnp.dot(combine, returned, preferred_element_type=jnp.float32)
+    mixed = lax.psum_scatter(routed, "dp", scatter_dimension=0, tiled=True)
     return mixed.astype(jnp.bfloat16)
 
 

time: 880 us -> 638 us (0.72)
  local copies, waits for them, and re-layouts: 228 us -> 2.51 us
  blocking collectives: 258 us -> 42.3 us
  waiting for transfers between devices: 268 us -> 423 us
  matrix products: 34.8 us -> 78.3 us
  starting transfers between devices: 5.34 us -> 45.6 us
  other arithmetic: 68.6 us -> 32.7 us
    all_to_all x1 -> x0, blocking collectives: 216 us -> none  [on_device(): lax.all_to_all(outgoing, 'expert', split_axis=1, concat_axis=1, tiled=True)]
    all_to_all x1 -> x4, waiting for transfers between devices: 196 us -> 356 us  [the longest x2 197 us: on_device(): received = lax.all_to_all(outgoing, 'expert', 0, 0, tiled=True)]
    gather x2 -> x0, local copies, waits for them, and re-layouts: 72.4 us -> none  [the longest x1 37.2 us: on_device(): returned.reshape(-1, model_width)[flat_index.reshape(-1)]]
    reshape x4 -> x0, local copies, waits for them, and re-layouts: 71.2 us -> none  [the longest x2 44.4 us: on_device(): padded[row_table]]
    convert_element_type x3 -> x0, local copies, waits for them, and re-layouts: 47.9 us -> none  [the longest x1 27.2 us: on_device(): picked.astype(jnp.float32)]
    dot_general x2 -> x8, matrix products: 23.1 us -> 71 us  [the longest x2 23.9 us: on_device(): jnp.dot(combine, returned, preferred_element_type=jnp.float32)]
    reduce_sum x1, other arithmetic: 54.1 us -> 11.7 us  [on_device(): jnp.sum(jnp.where(hit, all_gates[:, :, None], jnp.zeros((), jnp.bfloat16)...]
    all_to_all x1 -> x4, starting transfers between devices: 5.3 us -> 45.5 us  [the longest x2 23.6 us: on_device(): received = lax.all_to_all(outgoing, 'expert', 0, 0, tiled=True)]
  transfers between devices with their start and end apart: 3 -> 6, of which waited for: 2 -> 6; matrix products, arithmetic and copies ran while one was open for 3% -> 13% of each run, Pallas kernels for 0% -> 0%
where the time goes in v1:
time: 638 us
  waiting for transfers between devices  423 us (66%)
  matrix products  78.3 us (12%)
  starting transfers between devices  45.6 us (7%)
  blocking collectives  42.3 us (7%)
  other arithmetic  32.7 us (5%)
  between operations  13.6 us (2%)
    all_to_all x2, waiting for transfers between devices, on_device(): received = lax.all_to_all(outgoing, 'expert', 0, 0, tiled=True)  197 us
    all_to_all x2, waiting for transfers between devices, on_device(): returned = lax.all_to_all(partial_value, 'expert', 0, 0, tiled=True)  158 us
    reduce_scatter x1, waiting for transfers between devices, on_device(): mixed = lax.psum_scatter(routed, 'dp', scatter_dimension=0, tiled=True)  65.8 us
    dot_general x2, matrix products, on_device(): jnp.dot(combine, returned, preferred_element_type=jnp.float32)  23.9 us
    all_to_all x2, starting transfers between devices, on_device(): received = lax.all_to_all(outgoing, 'expert', 0, 0, tiled=True)  23.6 us
    all_gather x1, blocking collectives, on_device(): lax.all_gather(expert_ids, 'dp', axis=0, tiled=True)  23.3 us
    all_to_all x2, starting transfers between devices, on_device(): returned = lax.all_to_all(partial_value, 'expert', 0, 0, tiled=True)  22 us
    dot_general x2, matrix products, on_device(): lax.dot_general(dispatch, gathered, (((0,), (0,)), ((), ())), preferred_e...  19.6 us
  transfers between devices with their start and end apart: 6, of which 6 were waited for; matrix products, arithmetic and copies ran while one was open for 13% of the time, Pallas kernels for 0%

profile of v1, /device:TPU:1, one launch (start us, length us, event | category | flops | bytes accessed | tf_op | source)
XLA Modules:
  0.0 637.7 jit_solution(14678687119596894954)
XLA Ops:
  6.5 1.3 fusion.28
  7.8 1.9 fusion.30
  9.7 23.3 %all-gather = s32[8,64,6]{1,2,0:T(8,128)S(1)} all-gather(s32[1,64,6]{1,2,0:T(8,128)} %bitcast.59), channel_id=1, replica_groups=mesh['dp'=8,'expert'=32] {'dp'}, dimensions={0}, use_global_device_ids=true | all-gather | bytes 13824 | tf_op jit(solution)/shard_map/all_gather | solution.py:37
  33.6 7.2 %reduce-window.6 = s32[8,64,3,128]{3,1,2,0:T(8,128)S(1)} reduce-window(s32[8,64,3,128]{3,1,2,0:T(8,128)S(1)} %fusion.23, s32[]{:T(128)} %constant.50.clone.1), window={size=1x1x1x128 pad=0_0x0_0x0_0x127_0}, to_apply=%region_2.3 | reduce-window | flops 24969216 | bytes 1572868 | tf_op jit(solution)/shard_map/reduce-window
  40.8 0.3 slice.50
  41.1 0.9 copy.39
  42.0 0.7 fusion.38
  42.7 0.4 select_reduce_fusion
  43.9 7.7 %fusion.4 = (pred[512,1792]{1,0:T(8,128)(4,1)S(1)}, pred[512,1792]{1,0:T(8,128)(4,1)}) fusion(s32[512,6]{0,1:T(8,128)S(1)} %fusion.36, pred[512,6]{0,1:T(8,128)(4,1)S(1)} %get-tuple-element.12, pred[512,6]{0,1:T(8,128)(4,1)S(1)} %get-tuple-element.11), kind=kLoop, calls=%fused_computation.5 | loop fusion | flops 25690112 | bytes 1853440 | tf_op jit(solution)/shard_map/reduce_or | solution.py:64
  51.6 1.3 all-gather.4.cloned.1.call-done
  52.8 10.5 %convolution_convert_fusion.3 = bf16[1792,2560]{1,0:T(8,128)(2,1)} fusion(pred[512,1792]{1,0:T(8,128)(4,1)} %get-tuple-element.8, bf16[512,2560]{1,0:T(8,128)(2,1)} %all-gather.4.cloned.1.call-done), kind=kOutput, calls=%fused_computation.10 | convolution fusion | flops 4702208000 | bytes 12713984 | tf_op jit(solution)/shard_map/dot_general | solution.py:68
  63.4 12.7 %all-to-all-start = ((bf16[32,56,2560]{2,1,0:T(8,128)(2,1)}), bf16[32,56,2560]{2,1,0:T(8,128)(2,1)}, u32[]{:S(2)}, u32[]{:S(2)}) async-start(bf16[32,56,2560]{2,1,0:T(8,128)(2,1)} %bitcast.58), calls=%async_computation | async-start | bytes 18350080 | tf_op jit(solution)/shard_map/all_to_all | solution.py:71
  76.1 9.1 %convolution_convert_fusion.1 = bf16[1792,2560]{1,0:T(8,128)(2,1)} fusion(pred[512,1792]{1,0:T(8,128)(4,1)S(1)} %get-tuple-element.7, bf16[512,2560]{1,0:T(8,128)(2,1)} %all-gather.4.cloned.1.call-done), kind=kOutput, calls=%fused_computation.8 | convolution fusion | flops 4702208000 | bytes 12713984 | tf_op jit(solution)/shard_map/dot_general | solution.py:68
  85.2 101.0 %all-to-all-done = bf16[32,56,2560]{2,1,0:T(8,128)(2,1)} async-done(((bf16[32,56,2560]{2,1,0:T(8,128)(2,1)}), bf16[32,56,2560]{2,1,0:T(8,128)(2,1)}, u32[]{:S(2)}, u32[]{:S(2)}) %all-to-all-start) | async-done | bytes 9175072 | tf_op jit(solution)/shard_map/all_to_all | solution.py:71
  186.2 10.8 %all-to-all-start.2 = ((bf16[32,56,2560]{2,1,0:T(8,128)(2,1)}), bf16[32,56,2560]{2,1,0:T(8,128)(2,1)}, u32[]{:S(2)}, u32[]{:S(2)}) async-start(bf16[32,56,2560]{2,1,0:T(8,128)(2,1)} %bitcast.56), calls=%async_computation.2 | async-start | bytes 18350080 | tf_op jit(solution)/shard_map/all_to_all | solution.py:71
  197.1 7.6 %fusion.10 = f32[1792,384]{0,1:T(8,128)S(1)} fusion(bf16[1792,2560]{1,0:T(8,128)(2,1)} %bitcast.5, bf16[2,2560,384]{2,1,0:T(8,128)(2,1)} %param.14), kind=kOutput, calls=%fused_computation.17 | convolution fusion | flops 3523215360 | bytes 13893632 | tf_op jit(solution)/shard_map/dot_general | solution.py:72
  204.6 6.2 convolution_convert_fusion.2
  210.8 96.4 %all-to-all-done.2 = bf16[32,56,2560]{2,1,0:T(8,128)(2,1)} async-done(((bf16[32,56,2560]{2,1,0:T(8,128)(2,1)}), bf16[32,56,2560]{2,1,0:T(8,128)(2,1)}, u32[]{:S(2)}, u32[]{:S(2)}) %all-to-all-start.2) | async-done | bytes 9175072 | tf_op jit(solution)/shard_map/all_to_all | solution.py:71
  307.2 10.9 %all-to-all-start.1 = ((bf16[32,56,2560]{2,1,0:T(8,128)(2,1)}), bf16[32,56,2560]{2,1,0:T(8,128)(2,1)}, u32[]{:S(2)}, u32[]{:S(2)}) async-start(bf16[32,56,2560]{2,1,0:T(8,128)(2,1)} %bitcast.57), calls=%async_computation.1 | async-start | bytes 18350080 | tf_op jit(solution)/shard_map/all_to_all | solution.py:79
  318.1 7.6 %fusion.8 = f32[1792,384]{0,1:T(8,128)S(1)} fusion(bf16[1792,2560]{1,0:T(8,128)(2,1)} %bitcast.11, bf16[2,2560,384]{2,1,0:T(8,128)(2,1)} %param.14), kind=kOutput, calls=%fused_computation.15 | convolution fusion | flops 3523215360 | bytes 13893632 | tf_op jit(solution)/shard_map/dot_general | solution.py:72
  325.7 6.2 convolution_convert_fusion
  331.9 96.3 %all-to-all-done.1 = bf16[32,56,2560]{2,1,0:T(8,128)(2,1)} async-done(((bf16[32,56,2560]{2,1,0:T(8,128)(2,1)}), bf16[32,56,2560]{2,1,0:T(8,128)(2,1)}, u32[]{:S(2)}, u32[]{:S(2)}) %all-to-all-start.1) | async-done | bytes 9175072 | tf_op jit(solution)/shard_map/all_to_all | solution.py:79
  428.3 11.1 %all-to-all-start.3 = ((bf16[32,56,2560]{2,1,0:T(8,128)(2,1)}), bf16[32,56,2560]{2,1,0:T(8,128)(2,1)}, u32[]{:S(2)}, u32[]{:S(2)}) async-start(bf16[32,56,2560]{2,1,0:T(8,128)(2,1)} %bitcast.55), calls=%async_computation.3 | async-start | bytes 18350080 | tf_op jit(solution)/shard_map/all_to_all | solution.py:79
  439.4 19.0 %all-gather.1 = bf16[8,64,6]{1,2,0:T(8,128)(2,1)S(1)} all-gather(bf16[1,64,6]{1,2,0:T(8,128)(2,1)S(1)} %bitcast.60), channel_id=1, replica_groups=mesh['dp'=8,'expert'=32] {'dp'}, dimensions={0}, use_global_device_ids=true | all-gather | bytes 6912 | tf_op jit(solution)/shard_map/all_gather | solution.py:38
  458.4 11.7 %fusion.6 = (bf16[512,1792]{1,0:T(8,128)(2,1)}, bf16[512,1792]{1,0:T(8,128)(2,1)S(1)}) fusion(s32[512,6]{0,1:T(8,128)S(1)} %fusion.36, pred[512,6]{0,1:T(8,128)(4,1)S(1)} %get-tuple-element.12, bf16[512,6]{0,1:T(8,128)(2,1)S(1)} %reshape.122, pred[512,6]{0,1:T(8,128)(4,1)S(1)} %get-tuple-element.11), kind=kLoop, calls=%fused_computation.11 | loop fusion | flops 36700160 | bytes 3694592 | tf_op jit(solution)/shard_map/reduce_sum | solution.py:65
  470.2 4.3 fusion.44
  474.5 3.0 convolution_convert_fusion.4
  477.5 10.1 %fusion.45 = f32[512,2560]{1,0:T(8,128)} fusion(bf16[512,1792]{1,0:T(8,128)(2,1)S(1)} %get-tuple-element.6, bf16[1792,2560]{1,0:T(8,128)(2,1)} %bitcast.9), kind=kOutput, calls=%fused_computation.69 | convolution fusion | flops 4697620480 | bytes 16252928 | tf_op jit(solution)/shard_map/dot_general | solution.py:80
  487.6 61.8 %all-to-all-done.3 = bf16[32,56,2560]{2,1,0:T(8,128)(2,1)} async-done(((bf16[32,56,2560]{2,1,0:T(8,128)(2,1)}), bf16[32,56,2560]{2,1,0:T(8,128)(2,1)}, u32[]{:S(2)}, u32[]{:S(2)}) %all-to-all-start.3) | async-done | bytes 9175072 | tf_op jit(solution)/shard_map/all_to_all | solution.py:79
  549.5 13.7 %add_add_fusion = f32[512,2560]{1,0:T(8,128)} fusion(f32[512,2560]{1,0:T(8,128)} %fusion.45, bf16[512,2560]{1,0:T(8,128)(2,1)} %convolution_convert_fusion.4, bf16[512,1792]{1,0:T(8,128)(2,1)} %get-tuple-element.5, bf16[1792,2560]{1,0:T(8,128)(2,1)} %bitcast.15), kind=kOutput, calls=%fused_computation.13 | convolution fusion | flops 4701552640 | bytes 24117248 | tf_op jit(solution)/shard_map/dot_general | solution.py:80
  563.2 65.8 %reduce-scatter.2.cloned.1.call-done = f32[64,2560]{1,0:T(8,128)} async-done(((f32[512,2560]{1,0:T(8,128)}), f32[64,2560]{1,0:T(8,128)}) %reduce-scatter.2.cloned.1.call-update) | async-done | bytes 655376 | tf_op jit(solution)/shard_map/reduce_scatter | solution.py:81
  629.0 1.8 convert_element_type.59
  (34 shorter events, 1.6 us)
Async XLA Ops:
  6.5 467.9 %copy-start = (bf16[384,2560]{1,0:T(8,128)(2,1)S(1)}, bf16[384,2560]{1,0:T(8,128)(2,1)}, u32[]{:S(2)}) copy-start(bf16[384,2560]{1,0:T(8,128)(2,1)} %param.17) | copy-start | bytes 5898244
  6.5 46.3 %all-gather.4.cloned.1.call-start = ((), (), s32[]{:S(2)}) async-start(), calls=%async_computation.5 | async-start | bytes 2949120 | tf_op jit(solution)/shard_map/all_gather | solution.py:36
  33.2 9.5 %copy-start.2 = (s32[64]{0:T(128)S(1)}, s32[64]{0:T(128)}, u32[]{:S(2)}) copy-start(s32[64]{0:T(128)} %param.13) | copy-start | bytes 772
  63.4 122.8 %all-to-all-start = ((bf16[32,56,2560]{2,1,0:T(8,128)(2,1)}), bf16[32,56,2560]{2,1,0:T(8,128)(2,1)}, u32[]{:S(2)}, u32[]{:S(2)}) async-start(bf16[32,56,2560]{2,1,0:T(8,128)(2,1)} %bitcast.58), calls=%async_computation | async-start | bytes 18350080 | tf_op jit(solution)/shard_map/all_to_all | solution.py:71
  186.2 121.0 %all-to-all-start.2 = ((bf16[32,56,2560]{2,1,0:T(8,128)(2,1)}), bf16[32,56,2560]{2,1,0:T(8,128)(2,1)}, u32[]{:S(2)}, u32[]{:S(2)}) async-start(bf16[32,56,2560]{2,1,0:T(8,128)(2,1)} %bitcast.56), calls=%async_computation.2 | async-start | bytes 18350080 | tf_op jit(solution)/shard_map/all_to_all | solution.py:71
  197.0 7.6 %copy-start.4 = (bf16[2,192,2560]{2,1,0:T(8,128)(2,1)S(1)}, bf16[2,192,2560]{2,1,0:T(8,128)(2,1)}, u32[]{:S(2)}) copy-start(bf16[2,192,2560]{2,1,0:T(8,128)(2,1)} %param.15) | copy-start | bytes 5898244
  307.2 121.1 %all-to-all-start.1 = ((bf16[32,56,2560]{2,1,0:T(8,128)(2,1)}), bf16[32,56,2560]{2,1,0:T(8,128)(2,1)}, u32[]{:S(2)}, u32[]{:S(2)}) async-start(bf16[32,56,2560]{2,1,0:T(8,128)(2,1)} %bitcast.57), calls=%async_computation.1 | async-start | bytes 18350080 | tf_op jit(solution)/shard_map/all_to_all | solution.py:79
  318.1 7.6 %copy-start.5 = (bf16[2,192,2560]{2,1,0:T(8,128)(2,1)S(1)}, bf16[2,192,2560]{2,1,0:T(8,128)(2,1)}, u32[]{:S(2)}) copy-start(bf16[2,192,2560]{2,1,0:T(8,128)(2,1)} %param.15) | copy-start | bytes 5898244
  428.3 11.1 %copy-start.1 = (bf16[64,6]{0,1:T(8,128)(2,1)S(1)}, bf16[64,6]{0,1:T(8,128)(2,1)}, u32[]{:S(2)}) copy-start(bf16[64,6]{0,1:T(8,128)(2,1)} %param.12) | copy-start | bytes 2308
  428.3 121.2 %all-to-all-start.3 = ((bf16[32,56,2560]{2,1,0:T(8,128)(2,1)}), bf16[32,56,2560]{2,1,0:T(8,128)(2,1)}, u32[]{:S(2)}, u32[]{:S(2)}) async-start(bf16[32,56,2560]{2,1,0:T(8,128)(2,1)} %bitcast.55), calls=%async_computation.3 | async-start | bytes 18350080 | tf_op jit(solution)/shard_map/all_to_all | solution.py:79
  439.3 189.7 %reduce-scatter.2.cloned.1.call-start = ((), (), s32[]{:S(2)}) async-start(), calls=%async_computation.6 | async-start | bytes 5898240 | tf_op jit(solution)/shard_map/reduce_scatter | solution.py:81
  458.4 11.7 %copy-start.3 = (bf16[512,2560]{1,0:T(8,128)(2,1)S(1)}, bf16[512,2560]{1,0:T(8,128)(2,1)}, u32[]{:S(2)}) copy-start(bf16[512,2560]{1,0:T(8,128)(2,1)} %all-gather.4.cloned.1.call-done) | copy-start | bytes 7864324
Sparse Core Ops, SparseCore 0:
  9.8 42.9 all-gather.3
  563.3 65.6 reduce-scatter.1

commit v2 on v1

v2 whole, which is shorter than its diff:
```python
import jax
import jax.numpy as jnp
from jax import lax
from jax.sharding import PartitionSpec as P

epsilon = 1e-06


def normalize(hidden, gain):
    widened = hidden.astype(jnp.float32)
    mean_square = jnp.mean(widened * widened, axis=-1, keepdims=True)
    return (widened * lax.rsqrt(mean_square + epsilon) * gain).astype(jnp.bfloat16)


def on_device(
    hidden_in,
    norm_gain,
    expert_ids,
    gate_weights,
    expert_slot,
    w_in,
    w_down,
    shared_in,
    shared_down,
):
    groups = lax.axis_size("dp")
    columns = lax.axis_size("expert")
    local_experts = w_in.shape[0]
    experts = local_experts * columns
    token_count = hidden_in.shape[0]
    top_count = expert_ids.shape[1]
    capacity = max(2, token_count * top_count * 7 // (6 * experts))
    row_total = groups * token_count
    normed = normalize(hidden_in, norm_gain)
    meta = jnp.concatenate([expert_ids.astype(jnp.bfloat16), gate_weights], axis=1)
    gathered = lax.all_gather(normed, "dp", axis=0, tiled=True)
    all_meta = lax.all_gather(meta, "dp", axis=0, tiled=True)
    all_routes = all_meta[:, :top_count].astype(jnp.int32)
    all_gates = all_meta[:, top_count:]
    shared_width = shared_down.shape[0]
    shared_both = jnp.dot(gathered, shared_in, preferred_element_type=jnp.float32)
    shared_act = (
        jax.nn.silu(shared_both[:, :shared_width]) * shared_both[:, shared_width:]
    ).astype(jnp.bfloat16)
    shared_part = jnp.dot(shared_act, shared_down, preferred_element_type=jnp.float32).astype(
        jnp.bfloat16
    )
    slice_width = w_down.shape[1]

    def routes_of(routes, block_count):
        block_routes = routes.reshape(block_count, token_count * top_count)
        onehot = block_routes[:, :, None] == jnp.arange(experts, dtype=jnp.int32)[None, None, :]
        onehot_int = onehot.astype(jnp.int32)
        slot_rank = jnp.sum(jnp.cumsum(onehot_int, axis=1) * onehot_int, axis=2) - 1
        slot_of = jnp.sum(jnp.where(onehot, expert_slot[None, None, :], 0), axis=2)
        return slot_of // local_experts, slot_of % local_experts, slot_rank

    def expert_block(rows, local):
        gate_up = jnp.dot(rows, w_in[local], preferred_element_type=jnp.float32)
        activated = (
            jax.nn.silu(gate_up[:, :slice_width]) * gate_up[:, slice_width:]
        ).astype(jnp.bfloat16)
        return jnp.dot(activated, w_down[local], preferred_element_type=jnp.float32).astype(
            jnp.bfloat16
        )

    def one_hots(position, local_of, gates, local, buffer_rows):
        row_iota = jnp.arange(buffer_rows, dtype=jnp.int32)[None, None, :]
        hit = (position[:, :, None] == row_iota) & (local_of[:, :, None] == local)
        dispatch = jnp.any(hit, axis=1).astype(jnp.bfloat16)
        combine = jnp.sum(
            jnp.where(hit, gates[:, :, None], jnp.zeros((), jnp.bfloat16)), axis=1
        ).astype(jnp.bfloat16)
        return dispatch, combine

    dest_col, local_of, slot_rank = routes_of(all_routes, groups)
    group_of = jnp.arange(groups, dtype=jnp.int32)[:, None]
    position = ((dest_col * groups + group_of) * capacity + slot_rank).reshape(row_total, top_count)
    local_of = local_of.reshape(row_total, top_count)
    routed = shared_part.astype(jnp.float32)
    for local in range(local_experts - 1):
        dispatch, combine = one_hots(position, local_of, all_gates, local, columns * groups * capacity)
        outgoing = lax.dot_general(
            dispatch, gathered, (((0,), (0,)), ((), ())), preferred_element_type=jnp.float32
        ).astype(jnp.bfloat16)
        received = lax.all_to_all(outgoing, "expert", 0, 0, tiled=True)
        returned = lax.all_to_all(expert_block(received, local), "expert", 0, 0, tiled=True)
        routed = routed + jnp.dot(combine, returned, preferred_element_type=jnp.float32)
    last = local_experts - 1
    own_col, own_local, own_rank = routes_of(expert_ids, 1)
    own_position = (own_col * capacity + own_rank).reshape(token_count, top_count)
    own_local = own_local.reshape(token_count, top_count)
    dispatch, combine = one_hots(own_position, own_local, gate_weights, last, columns * capacity)
    outgoing = lax.dot_general(
        dispatch, normed, (((0,), (0,)), ((), ())), preferred_element_type=jnp.float32
    ).astype(jnp.bfloat16)
    received = lax.all_to_all(outgoing, "expert", 0, 0, tiled=True)
    spread = lax.all_gather(received, "dp", axis=0, tiled=True)
    summed = lax.psum_scatter(expert_block(spread, last), "dp", scatter_dimension=0, tiled=True)
    returned = lax.all_to_all(summed, "expert", 0, 0, tiled=True)
    own_routed = jnp.dot(combine, returned, preferred_element_type=jnp.float32)
    mixed = lax.psum_scatter(routed, "dp", scatter_dimension=0, tiled=True) + own_routed
    return mixed.astype(jnp.bfloat16)


def solution(mesh):
    return jax.shard_map(
        on_device,
        mesh=mesh,
        in_specs=(
            P(("dp", "expert"), None),
            P(),
            P(("dp", "expert"), None),
            P(("dp", "expert"), None),
            P(),
            P("expert", None, "dp"),
            P("expert", "dp", None),
            P(None, "dp"),
            P("dp", None),
        ),
        out_specs=P(("dp", "expert"), None),
        check_vma=False,
    )
```

time: 638 us -> 441 us (0.69)
  waiting for transfers between devices: 423 us -> 242 us
  matrix products: 78.3 us -> 62.1 us
  starting transfers between devices: 45.6 us -> 33 us
  local copies, waits for them, and re-layouts: 2.51 us -> 12 us
  blocking collectives: 42.3 us -> 50.5 us
    all_to_all x2 -> x1, waiting for transfers between devices: 197 us -> 47.1 us  [on_device(): received = lax.all_to_all(outgoing, 'expert', 0, 0, tiled=True)]
    all_gather x1 -> x2, waiting for transfers between devices: 1.26 us -> 49.1 us  [the longest x1 49.1 us: on_device(): spread = lax.all_gather(received, 'dp', axis=0, tiled=True)]
    all_to_all x2, waiting for transfers between devices: 158 us -> 113 us  [the longest x1 94.1 us: on_device(): lax.all_to_all(expert_block(received, local), 'expert', 0, 0, tiled=True)]
    reduce_scatter x1 -> x2, waiting for transfers between devices: 65.8 us -> 32.8 us  [the longest x1 32.8 us: on_device(): lax.psum_scatter(routed, 'dp', scatter_dimension=0, tiled=True) + own_routed]
    all_to_all x0 -> x1, blocking collectives: none -> 28.6 us  [on_device(): received = lax.all_to_all(outgoing, 'expert', 0, 0, tiled=True)]
    all_gather x2 -> x1, blocking collectives: 42.3 us -> 21.9 us  [on_device(): all_meta = lax.all_gather(meta, 'dp', axis=0, tiled=True)]
    all_to_all x2 -> x1, starting transfers between devices: 23.6 us -> 11.5 us  [on_device(): received = lax.all_to_all(outgoing, 'expert', 0, 0, tiled=True)]
    dot_general x2 -> x1, matrix products: 23.9 us -> 12.2 us  [on_device(): jnp.dot(combine, returned, preferred_element_type=jnp.float32)]
  transfers between devices with their start and end apart: 6 -> 7, of which waited for: 6 -> 5; matrix products, arithmetic and copies ran while one was open for 13% -> 20% of each run, Pallas kernels for 0% -> 0%
where the time goes in v2:
time: 441 us; the launch traced here: 440 us
  waiting for transfers between devices  242 us (55%)
  matrix products  62.1 us (14%)
  blocking collectives  50.5 us (11%)
  starting transfers between devices  33 us (7%)
  other arithmetic  27 us (6%)
  between operations  13.5 us (3%)
  local copies, waits for them, and re-layouts  12 us (3%)
    all_to_all x1, waiting for transfers between devices, on_device(): lax.all_to_all(expert_block(received, local), 'expert', 0, 0, tiled=True)  94.1 us
    all_gather x1, waiting for transfers between devices, on_device(): spread = lax.all_gather(received, 'dp', axis=0, tiled=True)  49.1 us
    all_to_all x1, waiting for transfers between devices, on_device(): received = lax.all_to_all(outgoing, 'expert', 0, 0, tiled=True)  47.1 us
    reduce_scatter x1, waiting for transfers between devices, on_device(): lax.psum_scatter(routed, 'dp', scatter_dimension=0, tiled=True) + own_routed  32.8 us
    all_to_all x1, blocking collectives, on_device(): received = lax.all_to_all(outgoing, 'expert', 0, 0, tiled=True)  28.6 us
    all_gather x1, blocking collectives, on_device(): all_meta = lax.all_gather(meta, 'dp', axis=0, tiled=True)  21.9 us
    all_to_all x1, waiting for transfers between devices, on_device(): returned = lax.all_to_all(summed, 'expert', 0, 0, tiled=True)  19.1 us
    dot_general x2, matrix products, expert_block(): gate_up = jnp.dot(rows, w_in[local], preferred_element_type=jnp.float32)  15.2 us
  transfers between devices with their start and end apart: 7, of which 5 were waited for; matrix products, arithmetic and copies ran while one was open for 20% of the time, Pallas kernels for 0%

profile of v2, /device:TPU:1, one launch (start us, length us, event | category | flops | bytes accessed | tf_op | source)
XLA Modules:
  0.0 440.3 jit_solution(3484238132043766241)
XLA Ops:
  6.5 1.3 fusion.25
  7.8 1.9 fusion.27
  10.7 0.9 reduce-window.16
  13.9 2.5 convolution_convert_fusion.4
  16.4 1.5 all_to_all.38
  17.9 28.6 %all_to_all.48 = bf16[32,7,2560]{2,1,0:T(8,128)(2,1)} all-to-all(bf16[32,7,2560]{2,1,0:T(8,128)(2,1)S(1)} %all_to_all.38), channel_id=1, replica_groups=mesh['dp'=8,'expert'=32] {'expert'}, dimensions={0} | all-to-all | bytes 2293760 | tf_op jit(solution)/shard_map/all_to_all | solution.py:97
  46.5 2.3 all_to_all.40
  48.9 21.9 %all-gather = bf16[8,64,12]{1,2,0:T(8,128)(2,1)S(1)} all-gather(bf16[1,64,12]{1,2,0:T(8,128)(2,1)S(1)} %maximum_bitcast_fusion), channel_id=1, replica_groups=mesh['dp'=8,'expert'=32] {'dp'}, dimensions={0}, use_global_device_ids=true | all-gather | bytes 13824 | tf_op jit(solution)/shard_map/all_gather | solution.py:37
  72.1 7.2 %reduce-window.14 = s32[8,64,3,128]{3,1,2,0:T(8,128)S(1)} reduce-window(s32[8,64,3,128]{3,1,2,0:T(8,128)S(1)} %fusion.20, s32[]{:T(128)} %constant.74.clone.1), window={size=1x1x1x128 pad=0_0x0_0x0_0x127_0}, to_apply=%region_2.3 | reduce-window | flops 24969216 | bytes 1572868 | tf_op jit(solution)/shard_map/reduce-window
  79.5 0.9 copy.68
  81.1 1.0 select_reduce_fusion
  83.0 4.6 %fusion.1 = pred[512,1792]{1,0:T(8,128)(4,1)S(1)} fusion(s32[512,6]{0,1:T(8,128)S(1)} %fusion.40, pred[512,6]{0,1:T(8,128)(4,1)S(1)} %fusion.41), kind=kLoop, calls=%fused_computation.2 | loop fusion | flops 15597568 | bytes 932864 | tf_op jit(solution)/shard_map/reduce_or | solution.py:70
  87.6 9.1 %convolution_convert_fusion.2 = bf16[1792,2560]{1,0:T(8,128)(2,1)} fusion(pred[512,1792]{1,0:T(8,128)(4,1)S(1)} %fusion.1, bf16[512,2560]{1,0:T(8,128)(2,1)} %all-gather.4.cloned.1.call-done), kind=kOutput, calls=%fused_computation.6 | convolution fusion | flops 4702208000 | bytes 12713984 | tf_op jit(solution)/shard_map/dot_general | solution.py:83
  96.7 11.5 %all-to-all-start = ((bf16[32,56,2560]{2,1,0:T(8,128)(2,1)}), bf16[32,56,2560]{2,1,0:T(8,128)(2,1)}, u32[]{:S(2)}, u32[]{:S(2)}) async-start(bf16[32,56,2560]{2,1,0:T(8,128)(2,1)} %bitcast.78), calls=%async_computation | async-start | bytes 18350080 | tf_op jit(solution)/shard_map/all_to_all | solution.py:86
  108.4 49.1 %all-gather.6.cloned.1.call-done = bf16[1792,2560]{1,0:T(8,128)(2,1)} async-done(((bf16[224,2560]{1,0:T(8,128)(2,1)}), bf16[1792,2560]{1,0:T(8,128)(2,1)}) %all-gather.6.cloned.1.call-update) | async-done | bytes 9175056 | tf_op jit(solution)/shard_map/all_gather | solution.py:98
  157.5 7.6 %fusion.5 = f32[1792,384]{0,1:T(8,128)S(1)} fusion(bf16[1792,2560]{1,0:T(8,128)(2,1)} %all-gather.6.cloned.1.call-done, bf16[2,2560,384]{2,1,0:T(8,128)(2,1)} %param.14), kind=kOutput, calls=%fused_computation.13 | convolution fusion | flops 3523215360 | bytes 13893632 | tf_op jit(solution)/shard_map/dot_general | solution.py:59
  165.1 6.1 %convolution_convert_fusion = bf16[1792,2560]{1,0:T(8,128)(2,1)} fusion(bf16[2,192,2560]{2,1,0:T(8,128)(2,1)S(1)} %copy-done.7, f32[1792,384]{0,1:T(8,128)S(1)} %fusion.5), kind=kOutput, calls=%fused_computation.4 | convolution fusion | flops 1768259584 | bytes 12910592 | tf_op jit(solution)/shard_map/dot_general | solution.py:63
  171.2 47.1 %all-to-all-done = bf16[32,56,2560]{2,1,0:T(8,128)(2,1)} async-done(((bf16[32,56,2560]{2,1,0:T(8,128)(2,1)}), bf16[32,56,2560]{2,1,0:T(8,128)(2,1)}, u32[]{:S(2)}, u32[]{:S(2)}) %all-to-all-start) | async-done | bytes 9175072 | tf_op jit(solution)/shard_map/all_to_all | solution.py:86
  218.3 7.7 %fusion.7 = f32[1792,384]{0,1:T(8,128)S(1)} fusion(bf16[1792,2560]{1,0:T(8,128)(2,1)} %bitcast.4, bf16[2,2560,384]{2,1,0:T(8,128)(2,1)} %param.14), kind=kOutput, calls=%fused_computation.15 | convolution fusion | flops 3523215360 | bytes 13893632 | tf_op jit(solution)/shard_map/dot_general | solution.py:59
  226.0 6.2 %convolution_convert_fusion.1 = bf16[1792,2560]{1,0:T(8,128)(2,1)} fusion(bf16[2,192,2560]{2,1,0:T(8,128)(2,1)S(1)} %copy-done.8, f32[1792,384]{0,1:T(8,128)S(1)} %fusion.7), kind=kOutput, calls=%fused_computation.5 | convolution fusion | flops 1768259584 | bytes 12910592 | tf_op jit(solution)/shard_map/dot_general | solution.py:63
  232.2 11.0 %all-to-all-start.1 = ((bf16[32,56,2560]{2,1,0:T(8,128)(2,1)}), bf16[32,56,2560]{2,1,0:T(8,128)(2,1)}, u32[]{:S(2)}, u32[]{:S(2)}) async-start(bf16[32,56,2560]{2,1,0:T(8,128)(2,1)} %bitcast.79), calls=%async_computation.1 | async-start | bytes 18350080 | tf_op jit(solution)/shard_map/all_to_all | solution.py:87
  243.5 7.6 %fusion.3 = bf16[512,1792]{1,0:T(8,128)(2,1)} fusion(s32[512,6]{0,1:T(8,128)S(1)} %fusion.40, pred[512,6]{0,1:T(8,128)(4,1)S(1)} %fusion.41, bf16[512,6]{0,1:T(8,128)(2,1)S(1)} %copy-done.1), kind=kLoop, calls=%fused_computation.7 | loop fusion | flops 21102592 | bytes 1856512 | tf_op jit(solution)/shard_map/reduce_sum | solution.py:71
  251.1 5.1 %fusion.56 = f32[512,768]{1,0:T(8,128)S(1)} fusion(bf16[512,2560]{1,0:T(8,128)(2,1)} %all-gather.4.cloned.1.call-done, bf16[2560,768]{1,0:T(8,128)(2,1)} %param.16), kind=kOutput, calls=%fused_computation.95 | convolution fusion | flops 2013265920 | bytes 8126464 | tf_op jit(solution)/shard_map/dot_general | solution.py:41
  256.2 3.1 convolution_convert_fusion.3
  259.3 94.1 %all-to-all-done.1 = bf16[32,56,2560]{2,1,0:T(8,128)(2,1)} async-done(((bf16[32,56,2560]{2,1,0:T(8,128)(2,1)}), bf16[32,56,2560]{2,1,0:T(8,128)(2,1)}, u32[]{:S(2)}, u32[]{:S(2)}) %all-to-all-start.1) | async-done | bytes 9175072 | tf_op jit(solution)/shard_map/all_to_all | solution.py:87
  353.4 12.2 %convert_add_fusion = f32[512,2560]{1,0:T(8,128)} fusion(bf16[512,2560]{1,0:T(8,128)(2,1)} %convolution_convert_fusion.3, bf16[512,1792]{1,0:T(8,128)(2,1)} %fusion.3, bf16[1792,2560]{1,0:T(8,128)(2,1)} %bitcast.8), kind=kOutput, calls=%fused_computation.8 | convolution fusion | flops 4700241920 | bytes 18874368 | tf_op jit(solution)/shard_map/dot_general | solution.py:88
  365.6 2.3 all_to_all.41
  367.9 10.0 %all-to-all-start.3 = ((bf16[32,7,2560]{2,1,0:T(8,128)(2,1)}), bf16[32,7,2560]{2,1,0:T(8,128)(2,1)S(1)}, u32[]{:S(2)}, u32[]{:S(2)}) async-start(bf16[32,7,2560]{2,1,0:T(8,128)(2,1)} %all_to_all.41), calls=%async_computation.5 | async-start | bytes 2621440 | tf_op jit(solution)/shard_map/all_to_all | solution.py:100
  378.1 19.1 %all-to-all-done.3 = bf16[32,7,2560]{2,1,0:T(8,128)(2,1)S(1)} async-done(((bf16[32,7,2560]{2,1,0:T(8,128)(2,1)}), bf16[32,7,2560]{2,1,0:T(8,128)(2,1)S(1)}, u32[]{:S(2)}, u32[]{:S(2)}) %all-to-all-start.3) | async-done | bytes 1146912 | tf_op jit(solution)/shard_map/all_to_all | solution.py:100
  397.3 1.2 all_to_all.43
  398.5 32.8 %reduce-scatter.3.cloned.1.call-done = f32[64,2560]{1,0:T(8,128)} async-done(((f32[512,2560]{1,0:T(8,128)}), f32[64,2560]{1,0:T(8,128)}) %reduce-scatter.3.cloned.1.call-update) | async-done | bytes 655376 | tf_op jit(solution)/shard_map/reduce_scatter | solution.py:102
  431.3 2.5 fusion.4
  (71 shorter events, 7.1 us)
Async XLA Ops:
  6.5 249.7 %copy-start = (bf16[384,2560]{1,0:T(8,128)(2,1)S(1)}, bf16[384,2560]{1,0:T(8,128)(2,1)}, u32[]{:S(2)}) copy-start(bf16[384,2560]{1,0:T(8,128)(2,1)} %param.17) | copy-start | bytes 5898244
  6.5 81.0 %all-gather.4.cloned.1.call-start = ((), (), s32[]{:S(2)}) async-start(), calls=%async_computation.6 | async-start | bytes 2949120 | tf_op jit(solution)/shard_map/all_gather | solution.py:36
  9.7 147.8 %all-gather.6.cloned.1.call-start = ((), (), s32[]{:S(2)}) async-start(), calls=%async_computation.8 | async-start | bytes 10321920 | tf_op jit(solution)/shard_map/all_gather | solution.py:98
  13.4 0.5 copy-start.3
  17.8 31.0 %copy-start.2 = (s32[64,6]{0,1:T(8,128)S(1)}, s32[64,6]{0,1:T(8,128)}, u32[]{:S(2)}) copy-start(s32[64,6]{0,1:T(8,128)} %param.11) | copy-start | bytes 4612
  17.9 31.0 %copy-start.5 = (bf16[64,6]{0,1:T(8,128)(2,1)S(1)}, bf16[64,6]{0,1:T(8,128)(2,1)}, u32[]{:S(2)}) copy-start(bf16[64,6]{0,1:T(8,128)(2,1)} %param.12) | copy-start | bytes 2308
  96.7 121.6 %all-to-all-start = ((bf16[32,56,2560]{2,1,0:T(8,128)(2,1)}), bf16[32,56,2560]{2,1,0:T(8,128)(2,1)}, u32[]{:S(2)}, u32[]{:S(2)}) async-start(bf16[32,56,2560]{2,1,0:T(8,128)(2,1)} %bitcast.78), calls=%async_computation | async-start | bytes 18350080 | tf_op jit(solution)/shard_map/all_to_all | solution.py:86
  108.2 257.4 %reduce-scatter.5.cloned.1.call-start = ((), (), s32[]{:S(2)}) async-start(), calls=%async_computation.9 | async-start | bytes 10321920 | tf_op jit(solution)/shard_map/reduce_scatter | solution.py:99
  157.5 7.6 %copy-start.7 = (bf16[2,192,2560]{2,1,0:T(8,128)(2,1)S(1)}, bf16[2,192,2560]{2,1,0:T(8,128)(2,1)}, u32[]{:S(2)}) copy-start(bf16[2,192,2560]{2,1,0:T(8,128)(2,1)} %param.15) | copy-start | bytes 5898244
  218.3 7.7 %copy-start.8 = (bf16[2,192,2560]{2,1,0:T(8,128)(2,1)S(1)}, bf16[2,192,2560]{2,1,0:T(8,128)(2,1)}, u32[]{:S(2)}) copy-start(bf16[2,192,2560]{2,1,0:T(8,128)(2,1)} %param.15) | copy-start | bytes 5898244
  232.2 11.3 %copy-start.1 = (bf16[512,6]{0,1:T(8,128)(2,1)S(1)}, bf16[512,6]{0,1:T(8,128)(2,1)}, u32[]{:S(2)}) copy-start(bf16[512,6]{0,1:T(8,128)(2,1)} %get-tuple-element.9) | copy-start | bytes 18436
  232.2 121.2 %all-to-all-start.1 = ((bf16[32,56,2560]{2,1,0:T(8,128)(2,1)}), bf16[32,56,2560]{2,1,0:T(8,128)(2,1)}, u32[]{:S(2)}, u32[]{:S(2)}) async-start(bf16[32,56,2560]{2,1,0:T(8,128)(2,1)} %bitcast.79), calls=%async_computation.1 | async-start | bytes 18350080 | tf_op jit(solution)/shard_map/all_to_all | solution.py:87
  243.2 188.0 %reduce-scatter.3.cloned.1.call-start = ((), (), s32[]{:S(2)}) async-start(), calls=%async_computation.7 | async-start | bytes 5898240 | tf_op jit(solution)/shard_map/reduce_scatter | solution.py:102
  365.5 12.3 %copy-start.4 = (pred[64,6]{0,1:T(8,128)(4,1)S(1)}, pred[64,6]{0,1:T(8,128)(4,1)}, u32[]{:S(2)}) copy-start(pred[64,6]{0,1:T(8,128)(4,1)} %copy-done.3) | copy-start | bytes 1156
  365.6 12.3 %copy-start.6 = (bf16[64,6]{0,1:T(8,128)(2,1)S(1)}, bf16[64,6]{0,1:T(8,128)(2,1)}, u32[]{:S(2)}) copy-start(bf16[64,6]{0,1:T(8,128)(2,1)} %param.12) | copy-start | bytes 2308
  367.9 29.4 %all-to-all-start.3 = ((bf16[32,7,2560]{2,1,0:T(8,128)(2,1)}), bf16[32,7,2560]{2,1,0:T(8,128)(2,1)S(1)}, u32[]{:S(2)}, u32[]{:S(2)}) async-start(bf16[32,7,2560]{2,1,0:T(8,128)(2,1)} %all_to_all.41), calls=%async_computation.5 | async-start | bytes 2621440 | tf_op jit(solution)/shard_map/all_to_all | solution.py:100
Sparse Core Ops, SparseCore 0:
  9.8 42.7 all-gather.3
  54.4 103.0 all-gather.5
  171.4 101.0 reduce-scatter.4
  365.7 65.5 reduce-scatter.2

commit v3 on v2

--- a/solution.py
+++ b/solution.py
@@ -32,9 +32,13 @@
     capacity = max(2, token_count * top_count * 7 // (6 * experts))
     row_total = groups * token_count
     normed = normalize(hidden_in, norm_gain)
+    model_width = hidden_in.shape[1]
     meta = jnp.concatenate([expert_ids.astype(jnp.bfloat16), gate_weights], axis=1)
-    gathered = lax.all_gather(normed, "dp", axis=0, tiled=True)
-    all_meta = lax.all_gather(meta, "dp", axis=0, tiled=True)
+    meta_row = jnp.zeros((1, model_width), jnp.bfloat16)
+    meta_row = meta_row.at[0, : token_count * 2 * top_count].set(meta.reshape(-1))
+    block = lax.all_gather(jnp.concatenate([normed, meta_row], axis=0), "dp", axis=0, tiled=False)
+    gathered = block[:, :token_count].reshape(row_total, model_width)
+    all_meta = block[:, token_count, : token_count * 2 * top_count].reshape(row_total, 2 * top_count)
     all_routes = all_meta[:, :top_count].astype(jnp.int32)
     all_gates = all_meta[:, top_count:]
     shared_width = shared_down.shape[0]
@@ -99,7 +103,8 @@
     summed = lax.psum_scatter(expert_block(spread, last), "dp", scatter_dimension=0, tiled=True)
     returned = lax.all_to_all(summed, "expert", 0, 0, tiled=True)
     own_routed = jnp.dot(combine, returned, preferred_element_type=jnp.float32)
-    mixed = lax.psum_scatter(routed, "dp", scatter_dimension=0, tiled=True) + own_routed
+    summed_rest = lax.psum_scatter(routed.astype(jnp.bfloat16), "dp", scatter_dimension=0, tiled=True)
+    mixed = summed_rest.astype(jnp.float32) + own_routed
     return mixed.astype(jnp.bfloat16)
 
 

time: 441 us -> 405 us (0.918)
  blocking collectives: 50.5 us -> 28.6 us
  waiting for transfers between devices: 242 us -> 224 us
    reduce_scatter x1, waiting for transfers between devices: 32.8 us -> 7.1 us  [on_device(): lax.psum_scatter(routed.astype(jnp.bfloat16), 'dp', scatter_dimension=0,...]
    all_gather x1 -> x0, blocking collectives: 21.9 us -> none  [on_device(): all_meta = lax.all_gather(meta, 'dp', axis=0, tiled=True)]
    all_to_all x1, waiting for transfers between devices: 47.1 us -> 29.8 us  [on_device(): received = lax.all_to_all(outgoing, 'expert', 0, 0, tiled=True)]
    all_gather x1, waiting for transfers between devices: 49.1 us -> 66.4 us  [on_device(): spread = lax.all_gather(received, 'dp', axis=0, tiled=True)]
    all_gather x1, waiting for transfers between devices: 0.02 us -> 7.86 us  [on_device(): lax.all_gather(jnp.concatenate([normed, meta_row], axis=0), 'dp', axis=0,...]
    another operation x5 -> x7, other arithmetic: 8.79 us -> 10.8 us
  transfers between devices with their start and end apart: 7 -> 7, of which waited for: 5 -> 6; matrix products, arithmetic and copies ran while one was open for 20% -> 22% of each run, Pallas kernels for 0% -> 0%
where the time goes in v3:
time: 405 us; the launch traced here: 401 us
  waiting for transfers between devices  224 us (55%)
  matrix products  58.4 us (14%)
  starting transfers between devices  30.6 us (8%)
  other arithmetic  29.1 us (7%)
  blocking collectives  28.6 us (7%)
  local copies, waits for them, and re-layouts  16.1 us (4%)
  between operations  13.5 us (3%)
    all_to_all x1, waiting for transfers between devices, on_device(): lax.all_to_all(expert_block(received, local), 'expert', 0, 0, tiled=True)  93.9 us
    all_gather x1, waiting for transfers between devices, on_device(): spread = lax.all_gather(received, 'dp', axis=0, tiled=True)  66.4 us
    all_to_all x1, waiting for transfers between devices, on_device(): received = lax.all_to_all(outgoing, 'expert', 0, 0, tiled=True)  29.8 us
    all_to_all x1, blocking collectives, on_device(): received = lax.all_to_all(outgoing, 'expert', 0, 0, tiled=True)  28.6 us
    all_to_all x1, waiting for transfers between devices, on_device(): returned = lax.all_to_all(summed, 'expert', 0, 0, tiled=True)  19.1 us
    dot_general x2, matrix products, expert_block(): gate_up = jnp.dot(rows, w_in[local], preferred_element_type=jnp.float32)  15.2 us
    dot_general x2, matrix products, expert_block(): jnp.dot(activated, w_down[local], preferred_element_type=jnp.float32)  12.4 us
    dot_general x1, matrix products, on_device(): jnp.dot(combine, returned, preferred_element_type=jnp.float32)  11.4 us
  transfers between devices with their start and end apart: 7, of which 6 were waited for; matrix products, arithmetic and copies ran while one was open for 22% of the time, Pallas kernels for 0%

profile of v3, /device:TPU:1, one launch (start us, length us, event | category | flops | bytes accessed | tf_op | source)
XLA Modules:
  0.0 400.6 jit_solution(18357418976481829318)
XLA Ops:
  7.2 1.1 fusion.26
  9.0 1.3 maximum_select_fusion
  10.6 1.1 fusion.28
  16.1 1.5 convolution_convert_fusion.4
  17.6 1.5 all_to_all.38
  19.0 28.6 %all_to_all.48 = bf16[32,7,2560]{2,1,0:T(8,128)(2,1)} all-to-all(bf16[32,7,2560]{2,1,0:T(8,128)(2,1)S(1)} %all_to_all.38), channel_id=1, replica_groups=mesh['dp'=8,'expert'=32] {'expert'}, dimensions={0} | all-to-all | bytes 2293760 | tf_op jit(solution)/shard_map/all_to_all | solution.py:101
  47.6 2.3 all_to_all.40
  50.6 7.9 %all-gather.7.cloned.1.call-done = bf16[8,65,2560]{2,1,0:T(8,128)(2,1)} async-done(((bf16[1,65,2560]{2,1,0:T(8,128)(2,1)}), bf16[8,65,2560]{2,1,0:T(8,128)(2,1)}) %all-gather.7.cloned.1.call-update) | async-done | bytes 2662416 | tf_op jit(solution)/shard_map/all_gather | solution.py:39
  60.9 7.2 %reduce-window.14 = s32[8,64,3,128]{3,1,2,0:T(8,128)S(1)} reduce-window(s32[8,64,3,128]{3,1,2,0:T(8,128)S(1)} %fusion.20, s32[]{:T(128)} %constant.101.clone.1), window={size=1x1x1x128 pad=0_0x0_0x0_0x127_0}, to_apply=%region_3.4 | reduce-window | flops 24969216 | bytes 1572868 | tf_op jit(solution)/shard_map/reduce-window
  70.0 1.0 select_reduce_fusion
  71.7 2.2 slice.88
  74.0 4.6 %fusion.1 = pred[512,1792]{1,0:T(8,128)(4,1)S(1)} fusion(s32[512,6]{0,1:T(8,128)S(1)} %fusion.43, pred[512,6]{0,1:T(8,128)(4,1)S(1)} %fusion.44), kind=kLoop, calls=%fused_computation.2 | loop fusion | flops 15597568 | bytes 932864 | tf_op jit(solution)/shard_map/reduce_or | solution.py:74
  78.5 7.3 %convolution_convert_fusion.2 = bf16[1792,2560]{1,0:T(8,128)(2,1)} fusion(pred[512,1792]{1,0:T(8,128)(4,1)S(1)} %fusion.1, bf16[512,2560]{1,0:T(8,128)(2,1)S(1)} %bitcast.79), kind=kOutput, calls=%fused_computation.6 | convolution fusion | flops 4702208000 | bytes 12713984 | tf_op jit(solution)/shard_map/dot_general | solution.py:87
  85.9 9.1 %all-to-all-start = ((bf16[32,56,2560]{2,1,0:T(8,128)(2,1)}), bf16[32,56,2560]{2,1,0:T(8,128)(2,1)}, u32[]{:S(2)}, u32[]{:S(2)}) async-start(bf16[32,56,2560]{2,1,0:T(8,128)(2,1)} %bitcast.77), calls=%async_computation | async-start | bytes 18350080 | tf_op jit(solution)/shard_map/all_to_all | solution.py:90
  95.3 66.4 %all-gather.5.cloned.1.call-done = bf16[1792,2560]{1,0:T(8,128)(2,1)} async-done(((bf16[224,2560]{1,0:T(8,128)(2,1)}), bf16[1792,2560]{1,0:T(8,128)(2,1)}) %all-gather.5.cloned.1.call-update) | async-done | bytes 9175056 | tf_op jit(solution)/shard_map/all_gather | solution.py:102
  161.7 7.6 %fusion.5 = f32[1792,384]{0,1:T(8,128)S(1)} fusion(bf16[1792,2560]{1,0:T(8,128)(2,1)} %all-gather.5.cloned.1.call-done, bf16[2,2560,384]{2,1,0:T(8,128)(2,1)} %param.16), kind=kOutput, calls=%fused_computation.13 | convolution fusion | flops 3523215360 | bytes 13893632 | tf_op jit(solution)/shard_map/dot_general | solution.py:63
  169.3 6.2 %convolution_convert_fusion = bf16[1792,2560]{1,0:T(8,128)(2,1)} fusion(bf16[2,192,2560]{2,1,0:T(8,128)(2,1)S(1)} %copy-done.8, f32[1792,384]{0,1:T(8,128)S(1)} %fusion.5), kind=kOutput, calls=%fused_computation.4 | convolution fusion | flops 1768259584 | bytes 12910592 | tf_op jit(solution)/shard_map/dot_general | solution.py:67
  175.4 29.8 %all-to-all-done = bf16[32,56,2560]{2,1,0:T(8,128)(2,1)} async-done(((bf16[32,56,2560]{2,1,0:T(8,128)(2,1)}), bf16[32,56,2560]{2,1,0:T(8,128)(2,1)}, u32[]{:S(2)}, u32[]{:S(2)}) %all-to-all-start) | async-done | bytes 9175072 | tf_op jit(solution)/shard_map/all_to_all | solution.py:90
  205.2 7.6 %fusion.7 = f32[1792,384]{0,1:T(8,128)S(1)} fusion(bf16[1792,2560]{1,0:T(8,128)(2,1)} %bitcast.5, bf16[2,2560,384]{2,1,0:T(8,128)(2,1)} %param.16), kind=kOutput, calls=%fused_computation.15 | convolution fusion | flops 3523215360 | bytes 13893632 | tf_op jit(solution)/shard_map/dot_general | solution.py:63
  212.9 6.2 %convolution_convert_fusion.1 = bf16[1792,2560]{1,0:T(8,128)(2,1)} fusion(bf16[2,192,2560]{2,1,0:T(8,128)(2,1)S(1)} %copy-done.9, f32[1792,384]{0,1:T(8,128)S(1)} %fusion.7), kind=kOutput, calls=%fused_computation.5 | convolution fusion | flops 1768259584 | bytes 12910592 | tf_op jit(solution)/shard_map/dot_general | solution.py:67
  219.1 11.0 %all-to-all-start.1 = ((bf16[32,56,2560]{2,1,0:T(8,128)(2,1)}), bf16[32,56,2560]{2,1,0:T(8,128)(2,1)}, u32[]{:S(2)}, u32[]{:S(2)}) async-start(bf16[32,56,2560]{2,1,0:T(8,128)(2,1)} %bitcast.78), calls=%async_computation.1 | async-start | bytes 18350080 | tf_op jit(solution)/shard_map/all_to_all | solution.py:91
  230.4 5.1 %fusion.59 = f32[512,768]{1,0:T(8,128)S(1)} fusion(bf16[512,2560]{1,0:T(8,128)(2,1)} %bitcast.80, bf16[2560,768]{1,0:T(8,128)(2,1)} %param.18), kind=kOutput, calls=%fused_computation.101 | convolution fusion | flops 2013265920 | bytes 8126464 | tf_op jit(solution)/shard_map/dot_general | solution.py:45
  235.6 3.1 convolution_convert_fusion.3
  238.7 7.6 %fusion.3 = bf16[512,1792]{1,0:T(8,128)(2,1)} fusion(s32[512,6]{0,1:T(8,128)S(1)} %fusion.43, pred[512,6]{0,1:T(8,128)(4,1)S(1)} %fusion.44, bf16[512,6]{0,1:T(8,128)(2,1)S(1)} %copy.60), kind=kLoop, calls=%fused_computation.7 | loop fusion | flops 21102592 | bytes 1856512 | tf_op jit(solution)/shard_map/reduce_sum | solution.py:75
  246.3 93.9 %all-to-all-done.1 = bf16[32,56,2560]{2,1,0:T(8,128)(2,1)} async-done(((bf16[32,56,2560]{2,1,0:T(8,128)(2,1)}), bf16[32,56,2560]{2,1,0:T(8,128)(2,1)}, u32[]{:S(2)}, u32[]{:S(2)}) %all-to-all-start.1) | async-done | bytes 9175072 | tf_op jit(solution)/shard_map/all_to_all | solution.py:91
  340.2 11.4 %add_convert_fusion = bf16[512,2560]{1,0:T(8,128)(2,1)} fusion(bf16[512,2560]{1,0:T(8,128)(2,1)} %convolution_convert_fusion.3, bf16[512,1792]{1,0:T(8,128)(2,1)} %fusion.3, bf16[1792,2560]{1,0:T(8,128)(2,1)} %bitcast.9), kind=kOutput, calls=%fused_computation.8 | convolution fusion | flops 4701552640 | bytes 16252928 | tf_op jit(solution)/shard_map/dot_general | solution.py:92
  351.7 2.3 all_to_all.41
  354.0 10.0 %all-to-all-start.3 = ((bf16[32,7,2560]{2,1,0:T(8,128)(2,1)}), bf16[32,7,2560]{2,1,0:T(8,128)(2,1)S(1)}, u32[]{:S(2)}, u32[]{:S(2)}) async-start(bf16[32,7,2560]{2,1,0:T(8,128)(2,1)} %all_to_all.41), calls=%async_computation.5 | async-start | bytes 2621440 | tf_op jit(solution)/shard_map/all_to_all | solution.py:104
  364.2 19.1 %all-to-all-done.3 = bf16[32,7,2560]{2,1,0:T(8,128)(2,1)S(1)} async-done(((bf16[32,7,2560]{2,1,0:T(8,128)(2,1)}), bf16[32,7,2560]{2,1,0:T(8,128)(2,1)S(1)}, u32[]{:S(2)}, u32[]{:S(2)}) %all-to-all-start.3) | async-done | bytes 1146912 | tf_op jit(solution)/shard_map/all_to_all | solution.py:104
  383.4 1.2 all_to_all.43
  384.6 7.1 %reduce-scatter.3.cloned.1.call-done = bf16[64,2560]{1,0:T(8,128)(2,1)} async-done(((bf16[512,2560]{1,0:T(8,128)(2,1)}), bf16[64,2560]{1,0:T(8,128)(2,1)}) %reduce-scatter.3.cloned.1.call-update) | async-done | bytes 327696 | tf_op jit(solution)/shard_map/reduce_scatter | solution.py:106
  391.7 2.4 fusion.4
  (77 shorter events, 12.3 us)
Async XLA Ops:
  6.5 229.0 %copy-start = (bf16[384,2560]{1,0:T(8,128)(2,1)S(1)}, bf16[384,2560]{1,0:T(8,128)(2,1)}, u32[]{:S(2)}) copy-start(bf16[384,2560]{1,0:T(8,128)(2,1)} %param.19) | copy-start | bytes 5898244
  6.5 8.4 %copy-start.7 = (s32[64]{0:T(128)S(1)}, s32[64]{0:T(128)}, u32[]{:S(2)}) copy-start(s32[64]{0:T(128)} %param.15) | copy-start | bytes 772
  6.5 51.9 %all-gather.7.cloned.1.call-start = ((), (), s32[]{:S(2)}) async-start(), calls=%async_computation.9 | async-start | bytes 3317760 | tf_op jit(solution)/shard_map/all_gather | solution.py:39
  12.5 149.2 %all-gather.5.cloned.1.call-start = ((), (), s32[]{:S(2)}) async-start(), calls=%async_computation.7 | async-start | bytes 10321920 | tf_op jit(solution)/shard_map/all_gather | solution.py:102
  15.5 0.5 copy-start.3
  71.7 2.3 copy-start.6
  73.9 12.0 %copy-start.1 = (bf16[8,64,2560]{2,1,0:T(8,128)(2,1)}, bf16[8,64,2560]{2,1,0:T(8,128)(2,1)S(1)}, u32[]{:S(2)}) copy-start(bf16[8,64,2560]{2,1,0:T(8,128)(2,1)S(1)} %slice.88) | copy-start | bytes 7864324
  85.9 119.3 %all-to-all-start = ((bf16[32,56,2560]{2,1,0:T(8,128)(2,1)}), bf16[32,56,2560]{2,1,0:T(8,128)(2,1)}, u32[]{:S(2)}, u32[]{:S(2)}) async-start(bf16[32,56,2560]{2,1,0:T(8,128)(2,1)} %bitcast.77), calls=%async_computation | async-start | bytes 18350080 | tf_op jit(solution)/shard_map/all_to_all | solution.py:90
  95.1 256.6 %reduce-scatter.5.cloned.1.call-start = ((), (), s32[]{:S(2)}) async-start(), calls=%async_computation.8 | async-start | bytes 10321920 | tf_op jit(solution)/shard_map/reduce_scatter | solution.py:103
  161.7 7.6 %copy-start.8 = (bf16[2,192,2560]{2,1,0:T(8,128)(2,1)S(1)}, bf16[2,192,2560]{2,1,0:T(8,128)(2,1)}, u32[]{:S(2)}) copy-start(bf16[2,192,2560]{2,1,0:T(8,128)(2,1)} %param.17) | copy-start | bytes 5898244
  205.2 7.6 %copy-start.9 = (bf16[2,192,2560]{2,1,0:T(8,128)(2,1)S(1)}, bf16[2,192,2560]{2,1,0:T(8,128)(2,1)}, u32[]{:S(2)}) copy-start(bf16[2,192,2560]{2,1,0:T(8,128)(2,1)} %param.17) | copy-start | bytes 5898244
  219.1 11.3 %copy-start.2 = (bf16[512,6]{1,0:T(8,128)(2,1)S(1)}, bf16[512,6]{1,0:T(8,128)(2,1)}, u32[]{:S(2)}) copy-start(bf16[512,6]{1,0:T(8,128)(2,1)} %get-tuple-element.21) | copy-start | bytes 18436
  219.1 121.1 %all-to-all-start.1 = ((bf16[32,56,2560]{2,1,0:T(8,128)(2,1)}), bf16[32,56,2560]{2,1,0:T(8,128)(2,1)}, u32[]{:S(2)}, u32[]{:S(2)}) async-start(bf16[32,56,2560]{2,1,0:T(8,128)(2,1)} %bitcast.78), calls=%async_computation.1 | async-start | bytes 18350080 | tf_op jit(solution)/shard_map/all_to_all | solution.py:91
  230.1 161.6 %reduce-scatter.3.cloned.1.call-start = ((), (), s32[]{:S(2)}) async-start(), calls=%async_computation.6 | async-start | bytes 2949120 | tf_op jit(solution)/shard_map/reduce_scatter | solution.py:106
  351.6 12.3 %copy-start.4 = (pred[64,6]{0,1:T(8,128)(4,1)S(1)}, pred[64,6]{0,1:T(8,128)(4,1)}, u32[]{:S(2)}) copy-start(pred[64,6]{0,1:T(8,128)(4,1)} %copy-done.3) | copy-start | bytes 1156
  351.7 12.3 %copy-start.5 = (bf16[64,6]{0,1:T(8,128)(2,1)S(1)}, bf16[64,6]{0,1:T(8,128)(2,1)}, u32[]{:S(2)}) copy-start(bf16[64,6]{0,1:T(8,128)(2,1)} %param.14) | copy-start | bytes 2308
  354.0 29.4 %all-to-all-start.3 = ((bf16[32,7,2560]{2,1,0:T(8,128)(2,1)}), bf16[32,7,2560]{2,1,0:T(8,128)(2,1)S(1)}, u32[]{:S(2)}, u32[]{:S(2)}) async-start(bf16[32,7,2560]{2,1,0:T(8,128)(2,1)} %all_to_all.41), calls=%async_computation.5 | async-start | bytes 2621440 | tf_op jit(solution)/shard_map/all_to_all | solution.py:104
Sparse Core Ops, SparseCore 0:
  12.6 45.7 all-gather.6
  60.2 101.3 all-gather.4
  175.6 101.0 reduce-scatter.4
  351.8 39.8 reduce-scatter.2

commit v4 on v3

--- a/solution.py
+++ b/solution.py
@@ -33,14 +33,29 @@
     row_total = groups * token_count
     normed = normalize(hidden_in, norm_gain)
     model_width = hidden_in.shape[1]
-    meta = jnp.concatenate([expert_ids.astype(jnp.bfloat16), gate_weights], axis=1)
+    def routes_of(routes, block_count):
+        block_routes = routes.reshape(block_count, token_count * top_count)
+        onehot = block_routes[:, :, None] == jnp.arange(experts, dtype=jnp.int32)[None, None, :]
+        onehot_int = onehot.astype(jnp.int32)
+        slot_rank = jnp.sum(jnp.cumsum(onehot_int, axis=1) * onehot_int, axis=2) - 1
+        slot_of = jnp.sum(jnp.where(onehot, expert_slot[None, None, :], 0), axis=2)
+        return slot_of, slot_rank
+
+    own_slot, own_rank = routes_of(expert_ids, 1)
+    own_slot = own_slot.reshape(token_count, top_count)
+    own_rank = own_rank.reshape(token_count, top_count)
+    meta = jnp.concatenate(
+        [own_slot.astype(jnp.bfloat16), own_rank.astype(jnp.bfloat16), gate_weights], axis=1
+    )
+    meta_width = token_count * 3 * top_count
     meta_row = jnp.zeros((1, model_width), jnp.bfloat16)
-    meta_row = meta_row.at[0, : token_count * 2 * top_count].set(meta.reshape(-1))
+    meta_row = meta_row.at[0, :meta_width].set(meta.reshape(-1))
     block = lax.all_gather(jnp.concatenate([normed, meta_row], axis=0), "dp", axis=0, tiled=False)
     gathered = block[:, :token_count].reshape(row_total, model_width)
-    all_meta = block[:, token_count, : token_count * 2 * top_count].reshape(row_total, 2 * top_count)
-    all_routes = all_meta[:, :top_count].astype(jnp.int32)
-    all_gates = all_meta[:, top_count:]
+    all_meta = block[:, token_count, :meta_width].reshape(row_total, 3 * top_count)
+    all_slots = all_meta[:, :top_count].astype(jnp.int32)
+    all_ranks = all_meta[:, top_count : 2 * top_count].astype(jnp.int32)
+    all_gates = all_meta[:, 2 * top_count :]
     shared_width = shared_down.shape[0]
     shared_both = jnp.dot(gathered, shared_in, preferred_element_type=jnp.float32)
     shared_act = (
@@ -50,14 +65,6 @@
         jnp.bfloat16
     )
     slice_width = w_down.shape[1]
-
-    def routes_of(routes, block_count):
-        block_routes = routes.reshape(block_count, token_count * top_count)
-        onehot = block_routes[:, :, None] == jnp.arange(experts, dtype=jnp.int32)[None, None, :]
-        onehot_int = onehot.astype(jnp.int32)
-        slot_rank = jnp.sum(jnp.cumsum(onehot_int, axis=1) * onehot_int, axis=2) - 1
-        slot_of = jnp.sum(jnp.where(onehot, expert_slot[None, None, :], 0), axis=2)
-        return slot_of // local_experts, slot_of % local_experts, slot_rank
 
     def expert_block(rows, local):
         gate_up = jnp.dot(rows, w_in[local], preferred_element_type=jnp.float32)
@@ -77,10 +84,9 @@
         ).astype(jnp.bfloat16)
         return dispatch, combine
 
-    dest_col, local_of, slot_rank = routes_of(all_routes, groups)
-    group_of = jnp.arange(groups, dtype=jnp.int32)[:, None]
-    position = ((dest_col * groups + group_of) * capacity + slot_rank).reshape(row_total, top_count)
-    local_of = local_of.reshape(row_total, top_count)
+    group_of = (jnp.arange(row_total, dtype=jnp.int32) // token_count)[:, None]
+    position = ((all_slots // local_experts) * groups + group_of) * capacity + all_ranks
+    local_of = all_slots % local_experts
     routed = shared_part.astype(jnp.float32)
     for local in range(local_experts - 1):
         dispatch, combine = one_hots(position, local_of, all_gates, local, columns * groups * capacity)
@@ -91,9 +97,8 @@
         returned = lax.all_to_all(expert_block(received, local), "expert", 0, 0, tiled=True)
         routed = routed + jnp.dot(combine, returned, preferred_element_type=jnp.float32)
     last = local_experts - 1
-    own_col, own_local, own_rank = routes_of(expert_ids, 1)
-    own_position = (own_col * capacity + own_rank).reshape(token_count, top_count)
-    own_local = own_local.reshape(token_count, top_count)
+    own_position = (own_slot // local_experts) * capacity + own_rank
+    own_local = own_slot % local_experts
     dispatch, combine = one_hots(own_position, own_local, gate_weights, last, columns * capacity)
     outgoing = lax.dot_general(
         dispatch, normed, (((0,), (0,)), ((), ())), preferred_element_type=jnp.float32

time: 405 us -> 396 us (0.978)
  other arithmetic: 29.1 us -> 19.3 us
    all_to_all x1, waiting for transfers between devices: 29.8 us -> 18.2 us  [on_device(): received = lax.all_to_all(outgoing, 'expert', 0, 0, tiled=True)]
    all_gather x1, waiting for transfers between devices: 66.4 us -> 77.9 us  [on_device(): spread = lax.all_gather(received, 'dp', axis=0, tiled=True)]
    another operation x7 -> x5, other arithmetic: 10.8 us -> 2.91 us
  transfers between devices with their start and end apart: 7 -> 7, of which waited for: 6 -> 6; matrix products, arithmetic and copies ran while one was open for 22% -> 19% of each run, Pallas kernels for 0% -> 0%
where the time goes in v4:
time: 396 us; the launch traced here: 392 us
  waiting for transfers between devices  228 us (58%)
  matrix products  58.4 us (15%)
  starting transfers between devices  30.8 us (8%)
  blocking collectives  28.6 us (7%)
  other arithmetic  19.3 us (5%)
  between operations  13.4 us (3%)
  local copies, waits for them, and re-layouts  13.3 us (3%)
    all_to_all x1, waiting for transfers between devices, on_device(): lax.all_to_all(expert_block(received, local), 'expert', 0, 0, tiled=True)  93.9 us
    all_gather x1, waiting for transfers between devices, on_device(): spread = lax.all_gather(received, 'dp', axis=0, tiled=True)  77.9 us
    all_to_all x1, blocking collectives, on_device(): received = lax.all_to_all(outgoing, 'expert', 0, 0, tiled=True)  28.6 us
    all_to_all x1, waiting for transfers between devices, on_device(): returned = lax.all_to_all(summed, 'expert', 0, 0, tiled=True)  19.2 us
    all_to_all x1, waiting for transfers between devices, on_device(): received = lax.all_to_all(outgoing, 'expert', 0, 0, tiled=True)  18.2 us
    dot_general x2, matrix products, expert_block(): gate_up = jnp.dot(rows, w_in[local], preferred_element_type=jnp.float32)  15.1 us
    dot_general x2, matrix products, expert_block(): jnp.dot(activated, w_down[local], preferred_element_type=jnp.float32)  12.4 us
    all_gather x1, waiting for transfers between devices, on_device(): lax.all_gather(jnp.concatenate([normed, meta_row], axis=0), 'dp', axis=0,...  11.6 us
  transfers between devices with their start and end apart: 7, of which 6 were waited for; matrix products, arithmetic and copies ran while one was open for 19% of the time, Pallas kernels for 0%

profile of v4, /device:TPU:1, one launch (start us, length us, event | category | flops | bytes accessed | tf_op | source)
XLA Modules:
  0.0 391.6 jit_solution(14193707251735526527)
XLA Ops:
  8.1 0.9 reduce-window.6
  10.8 1.4 maximum_select_fusion
  12.4 1.1 fusion.23
  13.6 1.1 fusion.25
  15.9 1.5 convolution_convert_fusion.4
  17.4 1.5 all_to_all.38
  18.9 28.6 %all_to_all.48 = bf16[32,7,2560]{2,1,0:T(8,128)(2,1)} all-to-all(bf16[32,7,2560]{2,1,0:T(8,128)(2,1)S(1)} %all_to_all.38), channel_id=1, replica_groups=mesh['dp'=8,'expert'=32] {'expert'}, dimensions={0} | all-to-all | bytes 2293760 | tf_op jit(solution)/shard_map/all_to_all | solution.py:106
  47.5 2.3 all_to_all.40
  49.8 11.6 %all-gather.7.cloned.1.call-done = bf16[8,65,2560]{2,1,0:T(8,128)(2,1)} async-done(((bf16[1,65,2560]{2,1,0:T(8,128)(2,1)}), bf16[8,65,2560]{2,1,0:T(8,128)(2,1)}) %all-gather.7.cloned.1.call-update) | async-done | bytes 2662416 | tf_op jit(solution)/shard_map/all_gather | solution.py:53
  61.4 1.0 slice_reduce_fusion.1
  63.1 2.0 slice.86
  65.1 4.6 %fusion.1 = pred[512,1792]{1,0:T(8,128)(4,1)S(1)} fusion(s32[512,6]{0,1:T(8,128)S(1)} %fusion.42, pred[512,6]{0,1:T(8,128)(4,1)S(1)} %fusion.43), kind=kLoop, calls=%fused_computation.2 | loop fusion | flops 15597568 | bytes 932864 | tf_op jit(solution)/shard_map/reduce_or | solution.py:81
  69.7 7.3 %convolution_convert_fusion.2 = bf16[1792,2560]{1,0:T(8,128)(2,1)} fusion(pred[512,1792]{1,0:T(8,128)(4,1)S(1)} %fusion.1, bf16[512,2560]{1,0:T(8,128)(2,1)S(1)} %bitcast.61), kind=kOutput, calls=%fused_computation.6 | convolution fusion | flops 4702208000 | bytes 12713984 | tf_op jit(solution)/shard_map/dot_general | solution.py:93
  77.1 9.4 %all-to-all-start = ((bf16[32,56,2560]{2,1,0:T(8,128)(2,1)}), bf16[32,56,2560]{2,1,0:T(8,128)(2,1)}, u32[]{:S(2)}, u32[]{:S(2)}) async-start(bf16[32,56,2560]{2,1,0:T(8,128)(2,1)} %bitcast.59), calls=%async_computation | async-start | bytes 18350080 | tf_op jit(solution)/shard_map/all_to_all | solution.py:96
  86.7 77.9 %all-gather.5.cloned.1.call-done = bf16[1792,2560]{1,0:T(8,128)(2,1)} async-done(((bf16[224,2560]{1,0:T(8,128)(2,1)}), bf16[1792,2560]{1,0:T(8,128)(2,1)}) %all-gather.5.cloned.1.call-update) | async-done | bytes 9175056 | tf_op jit(solution)/shard_map/all_gather | solution.py:107
  164.6 7.6 %fusion.5 = f32[1792,384]{0,1:T(8,128)S(1)} fusion(bf16[1792,2560]{1,0:T(8,128)(2,1)} %all-gather.5.cloned.1.call-done, bf16[2,2560,384]{2,1,0:T(8,128)(2,1)} %param.16), kind=kOutput, calls=%fused_computation.13 | convolution fusion | flops 3523215360 | bytes 13893632 | tf_op jit(solution)/shard_map/dot_general | solution.py:70
  172.2 6.2 %convolution_convert_fusion = bf16[1792,2560]{1,0:T(8,128)(2,1)} fusion(bf16[2,192,2560]{2,1,0:T(8,128)(2,1)S(1)} %copy-done.3, f32[1792,384]{0,1:T(8,128)S(1)} %fusion.5), kind=kOutput, calls=%fused_computation.4 | convolution fusion | flops 1768259584 | bytes 12910592 | tf_op jit(solution)/shard_map/dot_general | solution.py:74
  178.4 18.2 %all-to-all-done = bf16[32,56,2560]{2,1,0:T(8,128)(2,1)} async-done(((bf16[32,56,2560]{2,1,0:T(8,128)(2,1)}), bf16[32,56,2560]{2,1,0:T(8,128)(2,1)}, u32[]{:S(2)}, u32[]{:S(2)}) %all-to-all-start) | async-done | bytes 9175072 | tf_op jit(solution)/shard_map/all_to_all | solution.py:96
  196.6 7.6 %fusion.7 = f32[1792,384]{0,1:T(8,128)S(1)} fusion(bf16[1792,2560]{1,0:T(8,128)(2,1)} %bitcast.6, bf16[2,2560,384]{2,1,0:T(8,128)(2,1)} %param.16), kind=kOutput, calls=%fused_computation.15 | convolution fusion | flops 3523215360 | bytes 13893632 | tf_op jit(solution)/shard_map/dot_general | solution.py:70
  204.2 6.2 %convolution_convert_fusion.1 = bf16[1792,2560]{1,0:T(8,128)(2,1)} fusion(bf16[2,192,2560]{2,1,0:T(8,128)(2,1)S(1)} %copy-done.4, f32[1792,384]{0,1:T(8,128)S(1)} %fusion.7), kind=kOutput, calls=%fused_computation.5 | convolution fusion | flops 1768259584 | bytes 12910592 | tf_op jit(solution)/shard_map/dot_general | solution.py:74
  210.4 10.9 %all-to-all-start.1 = ((bf16[32,56,2560]{2,1,0:T(8,128)(2,1)}), bf16[32,56,2560]{2,1,0:T(8,128)(2,1)}, u32[]{:S(2)}, u32[]{:S(2)}) async-start(bf16[32,56,2560]{2,1,0:T(8,128)(2,1)} %bitcast.60), calls=%async_computation.1 | async-start | bytes 18350080 | tf_op jit(solution)/shard_map/all_to_all | solution.py:97
  221.7 5.1 %fusion.60 = f32[512,768]{1,0:T(8,128)S(1)} fusion(bf16[512,2560]{1,0:T(8,128)(2,1)} %bitcast.62, bf16[2560,768]{1,0:T(8,128)(2,1)} %param.18), kind=kOutput, calls=%fused_computation.101 | convolution fusion | flops 2013265920 | bytes 8126464 | tf_op jit(solution)/shard_map/dot_general | solution.py:60
  226.9 3.1 convolution_convert_fusion.3
  230.0 7.6 %fusion.3 = bf16[512,1792]{1,0:T(8,128)(2,1)} fusion(s32[512,6]{0,1:T(8,128)S(1)} %fusion.42, pred[512,6]{0,1:T(8,128)(4,1)S(1)} %fusion.43, bf16[512,6]{0,1:T(8,128)(2,1)S(1)} %copy.54), kind=kLoop, calls=%fused_computation.7 | loop fusion | flops 21102592 | bytes 1856512 | tf_op jit(solution)/shard_map/reduce_sum | solution.py:82
  237.6 93.9 %all-to-all-done.1 = bf16[32,56,2560]{2,1,0:T(8,128)(2,1)} async-done(((bf16[32,56,2560]{2,1,0:T(8,128)(2,1)}), bf16[32,56,2560]{2,1,0:T(8,128)(2,1)}, u32[]{:S(2)}, u32[]{:S(2)}) %all-to-all-start.1) | async-done | bytes 9175072 | tf_op jit(solution)/shard_map/all_to_all | solution.py:97
  331.5 11.4 %add_convert_fusion = bf16[512,2560]{1,0:T(8,128)(2,1)} fusion(bf16[512,2560]{1,0:T(8,128)(2,1)} %convolution_convert_fusion.3, bf16[512,1792]{1,0:T(8,128)(2,1)} %fusion.3, bf16[1792,2560]{1,0:T(8,128)(2,1)} %bitcast.10), kind=kOutput, calls=%fused_computation.8 | convolution fusion | flops 4701552640 | bytes 16252928 | tf_op jit(solution)/shard_map/dot_general | solution.py:98
  343.0 2.3 all_to_all.41
  345.3 10.0 %all-to-all-start.3 = ((bf16[32,7,2560]{2,1,0:T(8,128)(2,1)}), bf16[32,7,2560]{2,1,0:T(8,128)(2,1)S(1)}, u32[]{:S(2)}, u32[]{:S(2)}) async-start(bf16[32,7,2560]{2,1,0:T(8,128)(2,1)} %all_to_all.41), calls=%async_computation.5 | async-start | bytes 2621440 | tf_op jit(solution)/shard_map/all_to_all | solution.py:109
  355.5 19.2 %all-to-all-done.3 = bf16[32,7,2560]{2,1,0:T(8,128)(2,1)S(1)} async-done(((bf16[32,7,2560]{2,1,0:T(8,128)(2,1)}), bf16[32,7,2560]{2,1,0:T(8,128)(2,1)S(1)}, u32[]{:S(2)}, u32[]{:S(2)}) %all-to-all-start.3) | async-done | bytes 1146912 | tf_op jit(solution)/shard_map/all_to_all | solution.py:109
  374.7 1.2 all_to_all.43
  375.9 6.9 %reduce-scatter.3.cloned.1.call-done = bf16[64,2560]{1,0:T(8,128)(2,1)} async-done(((bf16[512,2560]{1,0:T(8,128)(2,1)}), bf16[64,2560]{1,0:T(8,128)(2,1)}) %reduce-scatter.3.cloned.1.call-update) | async-done | bytes 327696 | tf_op jit(solution)/shard_map/reduce_scatter | solution.py:111
  382.7 2.4 fusion.4
  (56 shorter events, 6.3 us)
Async XLA Ops:
  6.5 220.4 %copy-start = (bf16[384,2560]{1,0:T(8,128)(2,1)S(1)}, bf16[384,2560]{1,0:T(8,128)(2,1)}, u32[]{:S(2)}) copy-start(bf16[384,2560]{1,0:T(8,128)(2,1)} %param.19) | copy-start | bytes 5898244
  6.5 54.9 %all-gather.7.cloned.1.call-start = ((), (), s32[]{:S(2)}) async-start(), calls=%async_computation.9 | async-start | bytes 3317760 | tf_op jit(solution)/shard_map/all_gather | solution.py:53
  15.5 149.1 %all-gather.5.cloned.1.call-start = ((), (), s32[]{:S(2)}) async-start(), calls=%async_computation.7 | async-start | bytes 10321920 | tf_op jit(solution)/shard_map/all_gather | solution.py:107
  65.1 12.0 %copy-start.1 = (bf16[8,64,2560]{2,1,0:T(8,128)(2,1)}, bf16[8,64,2560]{2,1,0:T(8,128)(2,1)S(1)}, u32[]{:S(2)}) copy-start(bf16[8,64,2560]{2,1,0:T(8,128)(2,1)S(1)} %slice.86) | copy-start | bytes 7864324
  77.1 119.6 %all-to-all-start = ((bf16[32,56,2560]{2,1,0:T(8,128)(2,1)}), bf16[32,56,2560]{2,1,0:T(8,128)(2,1)}, u32[]{:S(2)}, u32[]{:S(2)}) async-start(bf16[32,56,2560]{2,1,0:T(8,128)(2,1)} %bitcast.59), calls=%async_computation | async-start | bytes 18350080 | tf_op jit(solution)/shard_map/all_to_all | solution.py:96
  86.5 256.5 %reduce-scatter.5.cloned.1.call-start = ((), (), s32[]{:S(2)}) async-start(), calls=%async_computation.8 | async-start | bytes 10321920 | tf_op jit(solution)/shard_map/reduce_scatter | solution.py:108
  164.6 7.6 %copy-start.3 = (bf16[2,192,2560]{2,1,0:T(8,128)(2,1)S(1)}, bf16[2,192,2560]{2,1,0:T(8,128)(2,1)}, u32[]{:S(2)}) copy-start(bf16[2,192,2560]{2,1,0:T(8,128)(2,1)} %param.17) | copy-start | bytes 5898244
  196.6 7.6 %copy-start.4 = (bf16[2,192,2560]{2,1,0:T(8,128)(2,1)S(1)}, bf16[2,192,2560]{2,1,0:T(8,128)(2,1)}, u32[]{:S(2)}) copy-start(bf16[2,192,2560]{2,1,0:T(8,128)(2,1)} %param.17) | copy-start | bytes 5898244
  210.4 121.1 %all-to-all-start.1 = ((bf16[32,56,2560]{2,1,0:T(8,128)(2,1)}), bf16[32,56,2560]{2,1,0:T(8,128)(2,1)}, u32[]{:S(2)}, u32[]{:S(2)}) async-start(bf16[32,56,2560]{2,1,0:T(8,128)(2,1)} %bitcast.60), calls=%async_computation.1 | async-start | bytes 18350080 | tf_op jit(solution)/shard_map/all_to_all | solution.py:97
  221.4 161.4 %reduce-scatter.3.cloned.1.call-start = ((), (), s32[]{:S(2)}) async-start(), calls=%async_computation.6 | async-start | bytes 2949120 | tf_op jit(solution)/shard_map/reduce_scatter | solution.py:111
  342.9 12.3 %copy-start.2 = (bf16[64,6]{0,1:T(8,128)(2,1)S(1)}, bf16[64,6]{0,1:T(8,128)(2,1)}, u32[]{:S(2)}) copy-start(bf16[64,6]{0,1:T(8,128)(2,1)} %param.14) | copy-start | bytes 2308
  345.3 29.4 %all-to-all-start.3 = ((bf16[32,7,2560]{2,1,0:T(8,128)(2,1)}), bf16[32,7,2560]{2,1,0:T(8,128)(2,1)S(1)}, u32[]{:S(2)}, u32[]{:S(2)}) async-start(bf16[32,7,2560]{2,1,0:T(8,128)(2,1)} %all_to_all.41), calls=%async_computation.5 | async-start | bytes 2621440 | tf_op jit(solution)/shard_map/all_to_all | solution.py:109
Sparse Core Ops, SparseCore 0:
  15.6 45.7 all-gather.6
  63.2 101.3 all-gather.4
  178.5 101.0 reduce-scatter.4
  343.1 39.6 reduce-scatter.2

commit v5 on v4

--- a/solution.py
+++ b/solution.py
@@ -87,15 +87,31 @@
     group_of = (jnp.arange(row_total, dtype=jnp.int32) // token_count)[:, None]
     position = ((all_slots // local_experts) * groups + group_of) * capacity + all_ranks
     local_of = all_slots % local_experts
-    routed = shared_part.astype(jnp.float32)
+    halves = 2
+    half_width = model_width // halves
+    summed_parts = []
     for local in range(local_experts - 1):
         dispatch, combine = one_hots(position, local_of, all_gates, local, columns * groups * capacity)
         outgoing = lax.dot_general(
             dispatch, gathered, (((0,), (0,)), ((), ())), preferred_element_type=jnp.float32
         ).astype(jnp.bfloat16)
         received = lax.all_to_all(outgoing, "expert", 0, 0, tiled=True)
-        returned = lax.all_to_all(expert_block(received, local), "expert", 0, 0, tiled=True)
-        routed = routed + jnp.dot(combine, returned, preferred_element_type=jnp.float32)
+        gate_up = jnp.dot(received, w_in[local], preferred_element_type=jnp.float32)
+        activated = (
+            jax.nn.silu(gate_up[:, :slice_width]) * gate_up[:, slice_width:]
+        ).astype(jnp.bfloat16)
+        for half in range(halves):
+            cols = slice(half * half_width, (half + 1) * half_width)
+            partial_value = jnp.dot(
+                activated, w_down[local][:, cols], preferred_element_type=jnp.float32
+            ).astype(jnp.bfloat16)
+            returned = lax.all_to_all(partial_value, "expert", 0, 0, tiled=True)
+            routed = shared_part[:, cols].astype(jnp.float32) + jnp.dot(
+                combine, returned, preferred_element_type=jnp.float32
+            )
+            summed_parts.append(
+                lax.psum_scatter(routed.astype(jnp.bfloat16), "dp", scatter_dimension=0, tiled=True)
+            )
     last = local_experts - 1
     own_position = (own_slot // local_experts) * capacity + own_rank
     own_local = own_slot % local_experts
@@ -108,7 +124,7 @@
     summed = lax.psum_scatter(expert_block(spread, last), "dp", scatter_dimension=0, tiled=True)
     returned = lax.all_to_all(summed, "expert", 0, 0, tiled=True)
     own_routed = jnp.dot(combine, returned, preferred_element_type=jnp.float32)
-    summed_rest = lax.psum_scatter(routed.astype(jnp.bfloat16), "dp", scatter_dimension=0, tiled=True)
+    summed_rest = jnp.concatenate(summed_parts, axis=1)
     mixed = summed_rest.astype(jnp.float32) + own_routed
     return mixed.astype(jnp.bfloat16)
 

time: 396 us -> 500 us (1.26)
  waiting for transfers between devices: 228 us -> 320 us
  local copies, waits for them, and re-layouts: 13.3 us -> 19 us
    all_to_all x1, waiting for transfers between devices: 18.2 us -> 108 us  [on_device(): received = lax.all_to_all(outgoing, 'expert', 0, 0, tiled=True)]
    dot_general x0 -> x3, matrix products: none -> 15.6 us  [the longest x2 8.18 us: on_device(): jnp.dot(activated, w_down[local][:, cols], preferred_element_type=jnp.flo...]
    all_gather x1, waiting for transfers between devices: 77.9 us -> 93.4 us  [on_device(): spread = lax.all_gather(received, 'dp', axis=0, tiled=True)]
    all_to_all x1 -> x2, waiting for transfers between devices: 93.9 us -> 84.1 us  [on_device(): returned = lax.all_to_all(partial_value, 'expert', 0, 0, tiled=True)]
    all_to_all x1 -> x2, starting transfers between devices: 10.9 us -> 19.2 us  [on_device(): returned = lax.all_to_all(partial_value, 'expert', 0, 0, tiled=True)]
    dot_general x2 -> x1, matrix products: 15.1 us -> 7.57 us  [expert_block(): gate_up = jnp.dot(rows, w_in[local], preferred_element_type=jnp.float32)]
    dot_general x2 -> x1, matrix products: 12.4 us -> 6.15 us  [expert_block(): jnp.dot(activated, w_down[local], preferred_element_type=jnp.float32)]
    dot_general x1 -> x2, matrix products: 11.4 us -> 12.8 us  [on_device(): jnp.dot(combine, returned, preferred_element_type=jnp.float32)]
  transfers between devices with their start and end apart: 7 -> 9, of which waited for: 6 -> 7; matrix products, arithmetic and copies ran while one was open for 19% -> 13% of each run, Pallas kernels for 0% -> 0%
where the time goes in v5:
time: 500 us; the launch traced here: 496 us
  waiting for transfers between devices  320 us (64%)
  matrix products  61.7 us (12%)
  starting transfers between devices  35.3 us (7%)
  blocking collectives  28.6 us (6%)
  local copies, waits for them, and re-layouts  19 us (4%)
  other arithmetic  18.5 us (4%)
  between operations  13.5 us (3%)
    all_to_all x1, waiting for transfers between devices, on_device(): received = lax.all_to_all(outgoing, 'expert', 0, 0, tiled=True)  108 us
    all_gather x1, waiting for transfers between devices, on_device(): spread = lax.all_gather(received, 'dp', axis=0, tiled=True)  93.4 us
    all_to_all x2, waiting for transfers between devices, on_device(): returned = lax.all_to_all(partial_value, 'expert', 0, 0, tiled=True)  84.1 us
    all_to_all x1, blocking collectives, on_device(): received = lax.all_to_all(outgoing, 'expert', 0, 0, tiled=True)  28.6 us
    all_to_all x2, starting transfers between devices, on_device(): returned = lax.all_to_all(partial_value, 'expert', 0, 0, tiled=True)  19.2 us
    all_to_all x1, waiting for transfers between devices, on_device(): returned = lax.all_to_all(summed, 'expert', 0, 0, tiled=True)  19.2 us
    dot_general x2, matrix products, on_device(): jnp.dot(combine, returned, preferred_element_type=jnp.float32)  12.8 us
    all_gather x1, waiting for transfers between devices, on_device(): lax.all_gather(jnp.concatenate([normed, meta_row], axis=0), 'dp', axis=0,...  11.4 us
  transfers between devices with their start and end apart: 9, of which 7 were waited for; matrix products, arithmetic and copies ran while one was open for 13% of the time, Pallas kernels for 0%

profile of v5, /device:TPU:1, one launch (start us, length us, event | category | flops | bytes accessed | tf_op | source)
XLA Modules:
  0.0 496.2 jit_solution(9057807556089066156)
XLA Ops:
  10.8 1.4 maximum_select_fusion
  15.9 1.5 convolution_convert_fusion.5
  17.5 1.5 all_to_all.49
  18.9 28.6 %all_to_all.60 = bf16[32,7,2560]{2,1,0:T(8,128)(2,1)} all-to-all(bf16[32,7,2560]{2,1,0:T(8,128)(2,1)S(1)} %all_to_all.49), channel_id=1, replica_groups=mesh['dp'=8,'expert'=32] {'expert'}, dimensions={0} | all-to-all | bytes 2293760 | tf_op jit(solution)/shard_map/all_to_all | solution.py:122
  47.5 2.3 all_to_all.51
  50.1 11.4 %all-gather.7.cloned.1.call-done = bf16[8,65,2560]{2,1,0:T(8,128)(2,1)} async-done(((bf16[1,65,2560]{2,1,0:T(8,128)(2,1)}), bf16[8,65,2560]{2,1,0:T(8,128)(2,1)}) %all-gather.7.cloned.1.call-update) | async-done | bytes 2662416 | tf_op jit(solution)/shard_map/all_gather | solution.py:53
  63.1 3.5 slice.103
  66.6 4.6 fusion.1
  71.2 93.4 %all-gather.5.cloned.1.call-done = bf16[1792,2560]{1,0:T(8,128)(2,1)} async-done(((bf16[224,2560]{1,0:T(8,128)(2,1)}), bf16[1792,2560]{1,0:T(8,128)(2,1)}) %all-gather.5.cloned.1.call-update) | async-done | bytes 9175056 | tf_op jit(solution)/shard_map/all_gather | solution.py:123
  164.6 7.6 %fusion.7 = f32[1792,384]{0,1:T(8,128)S(1)} fusion(bf16[1792,2560]{1,0:T(8,128)(2,1)} %all-gather.5.cloned.1.call-done, bf16[2,2560,384]{2,1,0:T(8,128)(2,1)} %param.16), kind=kOutput, calls=%fused_computation.17 | convolution fusion | flops 3523215360 | bytes 13893632 | tf_op jit(solution)/shard_map/dot_general | solution.py:70
  172.2 6.1 %convolution_convert_fusion = bf16[1792,2560]{1,0:T(8,128)(2,1)} fusion(bf16[2,192,2560]{2,1,0:T(8,128)(2,1)S(1)} %copy-done.3, f32[1792,384]{0,1:T(8,128)S(1)} %fusion.7), kind=kOutput, calls=%fused_computation.4 | convolution fusion | flops 1768259584 | bytes 12910592 | tf_op jit(solution)/shard_map/dot_general | solution.py:74
  178.4 9.1 %convolution_convert_fusion.1 = bf16[1792,2560]{1,0:T(8,128)(2,1)} fusion(pred[512,1792]{1,0:T(8,128)(4,1)S(1)} %fusion.1, bf16[512,2560]{1,0:T(8,128)(2,1)} %bitcast.67), kind=kOutput, calls=%fused_computation.5 | convolution fusion | flops 4702208000 | bytes 12713984 | tf_op jit(solution)/shard_map/dot_general | solution.py:95
  187.5 7.8 %all-to-all-start = ((bf16[32,56,2560]{2,1,0:T(8,128)(2,1)}), bf16[32,56,2560]{2,1,0:T(8,128)(2,1)}, u32[]{:S(2)}, u32[]{:S(2)}) async-start(bf16[32,56,2560]{2,1,0:T(8,128)(2,1)} %bitcast.66), calls=%async_computation | async-start | bytes 18350080 | tf_op jit(solution)/shard_map/all_to_all | solution.py:98
  195.2 2.2 slice_bitcast_fusion
  197.5 107.9 %all-to-all-done = bf16[32,56,2560]{2,1,0:T(8,128)(2,1)} async-done(((bf16[32,56,2560]{2,1,0:T(8,128)(2,1)}), bf16[32,56,2560]{2,1,0:T(8,128)(2,1)}, u32[]{:S(2)}, u32[]{:S(2)}) %all-to-all-start) | async-done | bytes 9175072 | tf_op jit(solution)/shard_map/all_to_all | solution.py:98
  305.3 7.4 %fusion.9 = f32[1792,384]{0,1:T(8,128)S(1)} fusion(bf16[1792,2560]{1,0:T(8,128)(2,1)} %bitcast.6, bf16[2,2560,384]{2,1,0:T(8,128)(2,1)} %param.16), kind=kOutput, calls=%fused_computation.19 | convolution fusion | flops 3523215360 | bytes 13893632 | tf_op jit(solution)/shard_map/dot_general | solution.py:99
  314.0 3.5 convolution_convert_fusion.3
  317.5 10.7 %all-to-all-start.1 = ((bf16[32,56,1280]{2,1,0:T(8,128)(2,1)}), bf16[32,56,1280]{2,1,0:T(8,128)(2,1)}, u32[]{:S(2)}, u32[]{:S(2)}) async-start(bf16[32,56,1280]{2,1,0:T(8,128)(2,1)} %bitcast.65), calls=%async_computation.1 | async-start | bytes 9175040 | tf_op jit(solution)/shard_map/all_to_all | solution.py:108
  328.3 4.6 convolution_convert_fusion.2
  332.9 50.1 %all-to-all-done.1 = bf16[32,56,1280]{2,1,0:T(8,128)(2,1)} async-done(((bf16[32,56,1280]{2,1,0:T(8,128)(2,1)}), bf16[32,56,1280]{2,1,0:T(8,128)(2,1)}, u32[]{:S(2)}, u32[]{:S(2)}) %all-to-all-start.1) | async-done | bytes 4587552 | tf_op jit(solution)/shard_map/all_to_all | solution.py:108
  383.0 8.5 %all-to-all-start.2 = ((bf16[32,56,1280]{2,1,0:T(8,128)(2,1)}), bf16[32,56,1280]{2,1,0:T(8,128)(2,1)}, u32[]{:S(2)}, u32[]{:S(2)}) async-start(bf16[32,56,1280]{2,1,0:T(8,128)(2,1)} %bitcast.64), calls=%async_computation.3 | async-start | bytes 9175040 | tf_op jit(solution)/shard_map/all_to_all | solution.py:108
  391.9 5.1 %fusion.59 = f32[512,768]{1,0:T(8,128)S(1)} fusion(bf16[512,2560]{1,0:T(8,128)(2,1)} %bitcast.68, bf16[2560,768]{1,0:T(8,128)(2,1)} %param.18), kind=kOutput, calls=%fused_computation.104 | convolution fusion | flops 2013265920 | bytes 8126464 | tf_op jit(solution)/shard_map/dot_general | solution.py:60
  397.1 1.5 convolution_convert_fusion.4
  398.6 6.3 %fusion.3 = bf16[512,1792]{1,0:T(8,128)(2,1)S(1)} fusion(s32[512,6]{0,1:T(8,128)S(1)} %fusion.42, pred[512,6]{0,1:T(8,128)(4,1)S(1)} %fusion.43, bf16[512,6]{0,1:T(8,128)(2,1)S(1)} %copy.54), kind=kLoop, calls=%fused_computation.6 | loop fusion | flops 21102592 | bytes 1856512 | tf_op jit(solution)/shard_map/reduce_sum | solution.py:82
  406.3 5.9 %fusion.5 = bf16[512,1280]{1,0:T(8,128)(2,1)} fusion(bf16[512,1792]{1,0:T(8,128)(2,1)S(1)} %fusion.3, bf16[1792,1280]{1,0:T(8,128)(2,1)} %bitcast.10, bf16[512,2560]{1,0:T(8,128)(2,1)S(1)} %convolution_convert_fusion.4), kind=kOutput, calls=%fused_computation.15 | convolution fusion | flops 2350776320 | bytes 9043968 | tf_op jit(solution)/shard_map/dot_general | solution.py:109
  412.3 34.0 %all-to-all-done.2 = bf16[32,56,1280]{2,1,0:T(8,128)(2,1)} async-done(((bf16[32,56,1280]{2,1,0:T(8,128)(2,1)}), bf16[32,56,1280]{2,1,0:T(8,128)(2,1)}, u32[]{:S(2)}, u32[]{:S(2)}) %all-to-all-start.2) | async-done | bytes 4587552 | tf_op jit(solution)/shard_map/all_to_all | solution.py:108
  446.3 6.8 %fusion.6 = bf16[512,1280]{1,0:T(8,128)(2,1)} fusion(bf16[512,1792]{1,0:T(8,128)(2,1)} %copy-done.2, bf16[1792,1280]{1,0:T(8,128)(2,1)} %bitcast.12, bf16[512,2560]{1,0:T(8,128)(2,1)} %copy-done.5), kind=kOutput, calls=%fused_computation.16 | convolution fusion | flops 2350776320 | bytes 9043968 | tf_op jit(solution)/shard_map/dot_general | solution.py:109
  453.2 2.3 all_to_all.52
  455.5 7.7 %all-to-all-start.4 = ((bf16[32,7,2560]{2,1,0:T(8,128)(2,1)}), bf16[32,7,2560]{2,1,0:T(8,128)(2,1)S(1)}, u32[]{:S(2)}, u32[]{:S(2)}) async-start(bf16[32,7,2560]{2,1,0:T(8,128)(2,1)} %all_to_all.52), calls=%async_computation.7 | async-start | bytes 2621440 | tf_op jit(solution)/shard_map/all_to_all | solution.py:125
  463.4 19.2 %all-to-all-done.4 = bf16[32,7,2560]{2,1,0:T(8,128)(2,1)S(1)} async-done(((bf16[32,7,2560]{2,1,0:T(8,128)(2,1)}), bf16[32,7,2560]{2,1,0:T(8,128)(2,1)S(1)}, u32[]{:S(2)}, u32[]{:S(2)}) %all-to-all-start.4) | async-done | bytes 1146912 | tf_op jit(solution)/shard_map/all_to_all | solution.py:125
  483.8 3.5 reduce-scatter.6.cloned.1.call-done
  487.3 2.4 fusion.4
  (67 shorter events, 14.2 us)
Async XLA Ops:
  6.5 390.5 %copy-start = (bf16[384,2560]{1,0:T(8,128)(2,1)S(1)}, bf16[384,2560]{1,0:T(8,128)(2,1)}, u32[]{:S(2)}) copy-start(bf16[384,2560]{1,0:T(8,128)(2,1)} %param.19) | copy-start | bytes 5898244
  6.5 54.9 %all-gather.7.cloned.1.call-start = ((), (), s32[]{:S(2)}) async-start(), calls=%async_computation.12 | async-start | bytes 3317760 | tf_op jit(solution)/shard_map/all_gather | solution.py:53
  15.5 149.1 %all-gather.5.cloned.1.call-start = ((), (), s32[]{:S(2)}) async-start(), calls=%async_computation.10 | async-start | bytes 10321920 | tf_op jit(solution)/shard_map/all_gather | solution.py:123
  49.9 403.3 %reduce-scatter.8.cloned.1.call-start = ((), (), s32[]{:S(2)}) async-start(), calls=%async_computation.11 | async-start | bytes 10321920 | tf_op jit(solution)/shard_map/reduce_scatter | solution.py:124
  164.6 7.6 %copy-start.3 = (bf16[2,192,2560]{2,1,0:T(8,128)(2,1)S(1)}, bf16[2,192,2560]{2,1,0:T(8,128)(2,1)}, u32[]{:S(2)}) copy-start(bf16[2,192,2560]{2,1,0:T(8,128)(2,1)} %param.17) | copy-start | bytes 5898244
  187.5 117.9 %all-to-all-start = ((bf16[32,56,2560]{2,1,0:T(8,128)(2,1)}), bf16[32,56,2560]{2,1,0:T(8,128)(2,1)}, u32[]{:S(2)}, u32[]{:S(2)}) async-start(bf16[32,56,2560]{2,1,0:T(8,128)(2,1)} %bitcast.66), calls=%async_computation | async-start | bytes 18350080 | tf_op jit(solution)/shard_map/all_to_all | solution.py:98
  312.8 1.2 copy-start.1
  317.5 65.5 %all-to-all-start.1 = ((bf16[32,56,1280]{2,1,0:T(8,128)(2,1)}), bf16[32,56,1280]{2,1,0:T(8,128)(2,1)}, u32[]{:S(2)}, u32[]{:S(2)}) async-start(bf16[32,56,1280]{2,1,0:T(8,128)(2,1)} %bitcast.65), calls=%async_computation.1 | async-start | bytes 9175040 | tf_op jit(solution)/shard_map/all_to_all | solution.py:108
  383.0 63.2 %all-to-all-start.2 = ((bf16[32,56,1280]{2,1,0:T(8,128)(2,1)}), bf16[32,56,1280]{2,1,0:T(8,128)(2,1)}, u32[]{:S(2)}, u32[]{:S(2)}) async-start(bf16[32,56,1280]{2,1,0:T(8,128)(2,1)} %bitcast.64), calls=%async_computation.3 | async-start | bytes 9175040 | tf_op jit(solution)/shard_map/all_to_all | solution.py:108
  391.5 92.3 %reduce-scatter.4.cloned.1.call-start = ((), (), s32[]{:S(2)}) async-start(), calls=%async_computation.8 | async-start | bytes 1474560 | tf_op jit(solution)/shard_map/reduce_scatter | solution.py:113
  398.6 6.4 %copy-start.5 = (bf16[512,2560]{1,0:T(8,128)(2,1)}, bf16[512,2560]{1,0:T(8,128)(2,1)S(1)}, u32[]{:S(2)}) copy-start(bf16[512,2560]{1,0:T(8,128)(2,1)S(1)} %convolution_convert_fusion.4) | copy-start | bytes 7864324
  405.0 1.3 copy-start.2
  412.2 75.1 %reduce-scatter.6.cloned.1.call-start = ((), (), s32[]{:S(2)}) async-start(), calls=%async_computation.9 | async-start | bytes 1474560 | tf_op jit(solution)/shard_map/reduce_scatter | solution.py:113
  453.1 10.0 %copy-start.4 = (bf16[64,6]{0,1:T(8,128)(2,1)S(1)}, bf16[64,6]{0,1:T(8,128)(2,1)}, u32[]{:S(2)}) copy-start(bf16[64,6]{0,1:T(8,128)(2,1)} %param.14) | copy-start | bytes 2308
  455.5 27.1 %all-to-all-start.4 = ((bf16[32,7,2560]{2,1,0:T(8,128)(2,1)}), bf16[32,7,2560]{2,1,0:T(8,128)(2,1)S(1)}, u32[]{:S(2)}, u32[]{:S(2)}) async-start(bf16[32,7,2560]{2,1,0:T(8,128)(2,1)} %all_to_all.52), calls=%async_computation.7 | async-start | bytes 2621440 | tf_op jit(solution)/shard_map/all_to_all | solution.py:125
Sparse Core Ops, SparseCore 0:
  15.6 45.7 all-gather.6
  63.3 101.3 all-gather.4
  178.5 101.0 reduce-scatter.7
  412.3 34.5 reduce-scatter.3
  453.3 33.9 reduce-scatter.5

commit v6 on v4

--- a/solution.py
+++ b/solution.py
@@ -95,7 +95,7 @@
         ).astype(jnp.bfloat16)
         received = lax.all_to_all(outgoing, "expert", 0, 0, tiled=True)
         returned = lax.all_to_all(expert_block(received, local), "expert", 0, 0, tiled=True)
-        routed = routed + jnp.dot(combine, returned, preferred_element_type=jnp.float32)
+        combined, combine_a, returned_a = routed, combine, returned
     last = local_experts - 1
     own_position = (own_slot // local_experts) * capacity + own_rank
     own_local = own_slot % local_experts
@@ -108,7 +108,17 @@
     summed = lax.psum_scatter(expert_block(spread, last), "dp", scatter_dimension=0, tiled=True)
     returned = lax.all_to_all(summed, "expert", 0, 0, tiled=True)
     own_routed = jnp.dot(combine, returned, preferred_element_type=jnp.float32)
-    summed_rest = lax.psum_scatter(routed.astype(jnp.bfloat16), "dp", scatter_dimension=0, tiled=True)
+    half_width = model_width // 2
+    summed_parts = []
+    for half in range(2):
+        cols = slice(half * half_width, (half + 1) * half_width)
+        part = combined[:, cols] + jnp.dot(
+            combine_a, returned_a[:, cols], preferred_element_type=jnp.float32
+        )
+        summed_parts.append(
+            lax.psum_scatter(part.astype(jnp.bfloat16), "dp", scatter_dimension=0, tiled=True)
+        )
+    summed_rest = jnp.concatenate(summed_parts, axis=1)
     mixed = summed_rest.astype(jnp.float32) + own_routed
     return mixed.astype(jnp.bfloat16)
 

time: 396 us -> 428 us (1.081)
  waiting for transfers between devices: 228 us -> 256 us
    reduce_scatter x1 -> x2, waiting for transfers between devices: 6.86 us -> 36 us  [on_device(): lax.psum_scatter(part.astype(jnp.bfloat16), 'dp', scatter_dimension=0, ti...]
    dot_general x1 -> x2, matrix products: 11.4 us -> 14.5 us  [on_device(): jnp.dot(combine_a, returned_a[:, cols], preferred_element_type=jnp.float32)]
  transfers between devices with their start and end apart: 7 -> 8, of which waited for: 6 -> 6; matrix products, arithmetic and copies ran while one was open for 19% -> 18% of each run, Pallas kernels for 0% -> 0%
where the time goes in v6:
time: 428 us; the launch traced here: 424 us
  waiting for transfers between devices  256 us (60%)
  matrix products  62.3 us (15%)
  starting transfers between devices  30.9 us (7%)
  blocking collectives  28.6 us (7%)
  other arithmetic  19.3 us (5%)
  between operations  13.4 us (3%)
  local copies, waits for them, and re-layouts  13.3 us (3%)
    all_to_all x1, waiting for transfers between devices, on_device(): lax.all_to_all(expert_block(received, local), 'expert', 0, 0, tiled=True)  93.1 us
    all_gather x1, waiting for transfers between devices, on_device(): spread = lax.all_gather(received, 'dp', axis=0, tiled=True)  77.9 us
    reduce_scatter x2, waiting for transfers between devices, on_device(): lax.psum_scatter(part.astype(jnp.bfloat16), 'dp', scatter_dimension=0, ti...  36 us
    all_to_all x1, blocking collectives, on_device(): received = lax.all_to_all(outgoing, 'expert', 0, 0, tiled=True)  28.6 us
    all_to_all x1, waiting for transfers between devices, on_device(): returned = lax.all_to_all(summed, 'expert', 0, 0, tiled=True)  19.2 us
    all_to_all x1, waiting for transfers between devices, on_device(): received = lax.all_to_all(outgoing, 'expert', 0, 0, tiled=True)  18.2 us
    dot_general x2, matrix products, expert_block(): gate_up = jnp.dot(rows, w_in[local], preferred_element_type=jnp.float32)  15.1 us
    dot_general x2, matrix products, on_device(): jnp.dot(combine_a, returned_a[:, cols], preferred_element_type=jnp.float32)  14.5 us
  transfers between devices with their start and end apart: 8, of which 6 were waited for; matrix products, arithmetic and copies ran while one was open for 18% of the time, Pallas kernels for 0%

profile of v6, /device:TPU:1, one launch (start us, length us, event | category | flops | bytes accessed | tf_op | source)
XLA Modules:
  0.0 423.9 jit_solution(10306052875272630769)
XLA Ops:
  10.8 1.4 maximum_select_fusion
  12.4 1.1 fusion.40
  13.6 1.1 fusion.42
  15.9 1.5 convolution_convert_fusion.4
  17.4 1.5 all_to_all.38
  18.9 28.6 %all_to_all.48 = bf16[32,7,2560]{2,1,0:T(8,128)(2,1)} all-to-all(bf16[32,7,2560]{2,1,0:T(8,128)(2,1)S(1)} %all_to_all.38), channel_id=1, replica_groups=mesh['dp'=8,'expert'=32] {'expert'}, dimensions={0} | all-to-all | bytes 2293760 | tf_op jit(solution)/shard_map/all_to_all | solution.py:106
  47.5 2.3 all_to_all.40
  49.8 11.6 %all-gather.7.cloned.1.call-done = bf16[8,65,2560]{2,1,0:T(8,128)(2,1)} async-done(((bf16[1,65,2560]{2,1,0:T(8,128)(2,1)}), bf16[8,65,2560]{2,1,0:T(8,128)(2,1)}) %all-gather.7.cloned.1.call-update) | async-done | bytes 2662416 | tf_op jit(solution)/shard_map/all_gather | solution.py:53
  61.4 1.0 slice_reduce_fusion.1
  63.1 2.0 slice.102
  65.1 4.6 %fusion.1 = pred[512,1792]{1,0:T(8,128)(4,1)S(1)} fusion(s32[512,6]{0,1:T(8,128)S(1)} %fusion.59, pred[512,6]{0,1:T(8,128)(4,1)S(1)} %fusion.60), kind=kLoop, calls=%fused_computation.2 | loop fusion | flops 15597568 | bytes 932864 | tf_op jit(solution)/shard_map/reduce_or | solution.py:81
  69.7 7.3 %convolution_convert_fusion.2 = bf16[1792,2560]{1,0:T(8,128)(2,1)} fusion(pred[512,1792]{1,0:T(8,128)(4,1)S(1)} %fusion.1, bf16[512,2560]{1,0:T(8,128)(2,1)S(1)} %bitcast.61), kind=kOutput, calls=%fused_computation.6 | convolution fusion | flops 4702208000 | bytes 12713984 | tf_op jit(solution)/shard_map/dot_general | solution.py:93
  77.1 9.4 %all-to-all-start = ((bf16[32,56,2560]{2,1,0:T(8,128)(2,1)}), bf16[32,56,2560]{2,1,0:T(8,128)(2,1)}, u32[]{:S(2)}, u32[]{:S(2)}) async-start(bf16[32,56,2560]{2,1,0:T(8,128)(2,1)} %bitcast.59), calls=%async_computation | async-start | bytes 18350080 | tf_op jit(solution)/shard_map/all_to_all | solution.py:96
  86.7 77.9 %all-gather.5.cloned.1.call-done = bf16[1792,2560]{1,0:T(8,128)(2,1)} async-done(((bf16[224,2560]{1,0:T(8,128)(2,1)}), bf16[1792,2560]{1,0:T(8,128)(2,1)}) %all-gather.5.cloned.1.call-update) | async-done | bytes 9175056 | tf_op jit(solution)/shard_map/all_gather | solution.py:107
  164.6 7.6 %fusion.22 = f32[1792,384]{0,1:T(8,128)S(1)} fusion(bf16[1792,2560]{1,0:T(8,128)(2,1)} %all-gather.5.cloned.1.call-done, bf16[2,2560,384]{2,1,0:T(8,128)(2,1)} %param.16), kind=kOutput, calls=%fused_computation.21 | convolution fusion | flops 3523215360 | bytes 13893632 | tf_op jit(solution)/shard_map/dot_general | solution.py:70
  172.2 6.2 %convolution_convert_fusion = bf16[1792,2560]{1,0:T(8,128)(2,1)} fusion(bf16[2,192,2560]{2,1,0:T(8,128)(2,1)S(1)} %copy-done.3, f32[1792,384]{0,1:T(8,128)S(1)} %fusion.22), kind=kOutput, calls=%fused_computation.4 | convolution fusion | flops 1768259584 | bytes 12910592 | tf_op jit(solution)/shard_map/dot_general | solution.py:74
  178.4 18.2 %all-to-all-done = bf16[32,56,2560]{2,1,0:T(8,128)(2,1)} async-done(((bf16[32,56,2560]{2,1,0:T(8,128)(2,1)}), bf16[32,56,2560]{2,1,0:T(8,128)(2,1)}, u32[]{:S(2)}, u32[]{:S(2)}) %all-to-all-start) | async-done | bytes 9175072 | tf_op jit(solution)/shard_map/all_to_all | solution.py:96
  196.6 7.6 %fusion.24 = f32[1792,384]{0,1:T(8,128)S(1)} fusion(bf16[1792,2560]{1,0:T(8,128)(2,1)} %bitcast.6, bf16[2,2560,384]{2,1,0:T(8,128)(2,1)} %param.16), kind=kOutput, calls=%fused_computation.23 | convolution fusion | flops 3523215360 | bytes 13893632 | tf_op jit(solution)/shard_map/dot_general | solution.py:70
  204.2 6.2 %convolution_convert_fusion.1 = bf16[1792,2560]{1,0:T(8,128)(2,1)} fusion(bf16[2,192,2560]{2,1,0:T(8,128)(2,1)S(1)} %copy-done.4, f32[1792,384]{0,1:T(8,128)S(1)} %fusion.24), kind=kOutput, calls=%fused_computation.5 | convolution fusion | flops 1768259584 | bytes 12910592 | tf_op jit(solution)/shard_map/dot_general | solution.py:74
  210.4 10.9 %all-to-all-start.1 = ((bf16[32,56,2560]{2,1,0:T(8,128)(2,1)}), bf16[32,56,2560]{2,1,0:T(8,128)(2,1)}, u32[]{:S(2)}, u32[]{:S(2)}) async-start(bf16[32,56,2560]{2,1,0:T(8,128)(2,1)} %bitcast.60), calls=%async_computation.1 | async-start | bytes 18350080 | tf_op jit(solution)/shard_map/all_to_all | solution.py:97
  221.7 5.1 %fusion.77 = f32[512,768]{1,0:T(8,128)S(1)} fusion(bf16[512,2560]{1,0:T(8,128)(2,1)} %bitcast.62, bf16[2560,768]{1,0:T(8,128)(2,1)} %param.18), kind=kOutput, calls=%fused_computation.109 | convolution fusion | flops 2013265920 | bytes 8126464 | tf_op jit(solution)/shard_map/dot_general | solution.py:60
  226.9 3.9 fusion.8
  230.8 7.6 %fusion.3 = bf16[512,1792]{1,0:T(8,128)(2,1)} fusion(s32[512,6]{0,1:T(8,128)S(1)} %fusion.59, pred[512,6]{0,1:T(8,128)(4,1)S(1)} %fusion.60, bf16[512,6]{0,1:T(8,128)(2,1)S(1)} %copy.54), kind=kLoop, calls=%fused_computation.7 | loop fusion | flops 21102592 | bytes 1856512 | tf_op jit(solution)/shard_map/reduce_sum | solution.py:82
  238.4 93.1 %all-to-all-done.1 = bf16[32,56,2560]{2,1,0:T(8,128)(2,1)} async-done(((bf16[32,56,2560]{2,1,0:T(8,128)(2,1)}), bf16[32,56,2560]{2,1,0:T(8,128)(2,1)}, u32[]{:S(2)}, u32[]{:S(2)}) %all-to-all-start.1) | async-done | bytes 9175072 | tf_op jit(solution)/shard_map/all_to_all | solution.py:97
  331.5 7.3 %fusion.19 = bf16[512,1280]{1,0:T(8,128)(2,1)} fusion(bf16[512,1792]{1,0:T(8,128)(2,1)} %fusion.3, bf16[1792,2560]{1,0:T(8,128)(2,1)} %bitcast.10, f32[512,2560]{1,0:T(8,128)} %fusion.8), kind=kOutput, calls=%fused_computation.20 | convolution fusion | flops 2350120960 | bytes 10354688 | tf_op jit(solution)/shard_map/dot_general | solution.py:115
  338.9 7.3 %fusion.16 = bf16[512,1280]{1,0:T(8,128)(2,1)} fusion(bf16[512,1792]{1,0:T(8,128)(2,1)} %fusion.3, bf16[1792,2560]{1,0:T(8,128)(2,1)} %bitcast.10, f32[512,2560]{1,0:T(8,128)} %fusion.8), kind=kOutput, calls=%fused_computation.19 | convolution fusion | flops 2350120960 | bytes 10354688 | tf_op jit(solution)/shard_map/dot_general | solution.py:115
  346.2 2.3 all_to_all.41
  348.5 10.0 %all-to-all-start.3 = ((bf16[32,7,2560]{2,1,0:T(8,128)(2,1)}), bf16[32,7,2560]{2,1,0:T(8,128)(2,1)S(1)}, u32[]{:S(2)}, u32[]{:S(2)}) async-start(bf16[32,7,2560]{2,1,0:T(8,128)(2,1)} %all_to_all.41), calls=%async_computation.6 | async-start | bytes 2621440 | tf_op jit(solution)/shard_map/all_to_all | solution.py:109
  358.7 19.2 %all-to-all-done.3 = bf16[32,7,2560]{2,1,0:T(8,128)(2,1)S(1)} async-done(((bf16[32,7,2560]{2,1,0:T(8,128)(2,1)}), bf16[32,7,2560]{2,1,0:T(8,128)(2,1)S(1)}, u32[]{:S(2)}, u32[]{:S(2)}) %all-to-all-start.3) | async-done | bytes 1146912 | tf_op jit(solution)/shard_map/all_to_all | solution.py:109
  377.9 1.2 all_to_all.43
  379.1 36.0 %reduce-scatter.6.cloned.1.call-done = bf16[64,1280]{1,0:T(8,128)(2,1)} async-done(((bf16[512,1280]{1,0:T(8,128)(2,1)}), bf16[64,1280]{1,0:T(8,128)(2,1)}) %reduce-scatter.6.cloned.1.call-update) | async-done | bytes 163856 | tf_op jit(solution)/shard_map/reduce_scatter | solution.py:119
  415.1 2.4 fusion.9
  (60 shorter events, 7.2 us)
Async XLA Ops:
  6.5 220.4 %copy-start = (bf16[384,2560]{1,0:T(8,128)(2,1)S(1)}, bf16[384,2560]{1,0:T(8,128)(2,1)}, u32[]{:S(2)}) copy-start(bf16[384,2560]{1,0:T(8,128)(2,1)} %param.19) | copy-start | bytes 5898244
  6.5 54.9 %all-gather.7.cloned.1.call-start = ((), (), s32[]{:S(2)}) async-start(), calls=%async_computation.11 | async-start | bytes 3317760 | tf_op jit(solution)/shard_map/all_gather | solution.py:53
  15.5 149.1 %all-gather.5.cloned.1.call-start = ((), (), s32[]{:S(2)}) async-start(), calls=%async_computation.9 | async-start | bytes 10321920 | tf_op jit(solution)/shard_map/all_gather | solution.py:107
  65.1 12.0 %copy-start.1 = (bf16[8,64,2560]{2,1,0:T(8,128)(2,1)}, bf16[8,64,2560]{2,1,0:T(8,128)(2,1)S(1)}, u32[]{:S(2)}) copy-start(bf16[8,64,2560]{2,1,0:T(8,128)(2,1)S(1)} %slice.102) | copy-start | bytes 7864324
  77.1 119.6 %all-to-all-start = ((bf16[32,56,2560]{2,1,0:T(8,128)(2,1)}), bf16[32,56,2560]{2,1,0:T(8,128)(2,1)}, u32[]{:S(2)}, u32[]{:S(2)}) async-start(bf16[32,56,2560]{2,1,0:T(8,128)(2,1)} %bitcast.59), calls=%async_computation | async-start | bytes 18350080 | tf_op jit(solution)/shard_map/all_to_all | solution.py:96
  86.5 259.7 %reduce-scatter.8.cloned.1.call-start = ((), (), s32[]{:S(2)}) async-start(), calls=%async_computation.10 | async-start | bytes 10321920 | tf_op jit(solution)/shard_map/reduce_scatter | solution.py:108
  164.6 7.6 %copy-start.3 = (bf16[2,192,2560]{2,1,0:T(8,128)(2,1)S(1)}, bf16[2,192,2560]{2,1,0:T(8,128)(2,1)}, u32[]{:S(2)}) copy-start(bf16[2,192,2560]{2,1,0:T(8,128)(2,1)} %param.17) | copy-start | bytes 5898244
  196.6 7.6 %copy-start.4 = (bf16[2,192,2560]{2,1,0:T(8,128)(2,1)S(1)}, bf16[2,192,2560]{2,1,0:T(8,128)(2,1)}, u32[]{:S(2)}) copy-start(bf16[2,192,2560]{2,1,0:T(8,128)(2,1)} %param.17) | copy-start | bytes 5898244
  210.4 121.1 %all-to-all-start.1 = ((bf16[32,56,2560]{2,1,0:T(8,128)(2,1)}), bf16[32,56,2560]{2,1,0:T(8,128)(2,1)}, u32[]{:S(2)}, u32[]{:S(2)}) async-start(bf16[32,56,2560]{2,1,0:T(8,128)(2,1)} %bitcast.60), calls=%async_computation.1 | async-start | bytes 18350080 | tf_op jit(solution)/shard_map/all_to_all | solution.py:97
  221.4 157.7 %reduce-scatter.4.cloned.1.call-start = ((), (), s32[]{:S(2)}) async-start(), calls=%async_computation.7 | async-start | bytes 1474560 | tf_op jit(solution)/shard_map/reduce_scatter | solution.py:119
  338.8 76.2 %reduce-scatter.6.cloned.1.call-start = ((), (), s32[]{:S(2)}) async-start(), calls=%async_computation.8 | async-start | bytes 1474560 | tf_op jit(solution)/shard_map/reduce_scatter | solution.py:119
  346.1 12.3 %copy-start.2 = (bf16[64,6]{0,1:T(8,128)(2,1)S(1)}, bf16[64,6]{0,1:T(8,128)(2,1)}, u32[]{:S(2)}) copy-start(bf16[64,6]{0,1:T(8,128)(2,1)} %param.14) | copy-start | bytes 2308
  348.5 29.4 %all-to-all-start.3 = ((bf16[32,7,2560]{2,1,0:T(8,128)(2,1)}), bf16[32,7,2560]{2,1,0:T(8,128)(2,1)S(1)}, u32[]{:S(2)}, u32[]{:S(2)}) async-start(bf16[32,7,2560]{2,1,0:T(8,128)(2,1)} %all_to_all.41), calls=%async_computation.6 | async-start | bytes 2621440 | tf_op jit(solution)/shard_map/all_to_all | solution.py:109
Sparse Core Ops, SparseCore 0:
  15.6 45.7 all-gather.6
  63.2 101.3 all-gather.4
  178.5 101.0 reduce-scatter.7
  338.9 35.1 reduce-scatter.3
  376.5 38.4 reduce-scatter.5
